TPU v7x, 1024 devices: a whole 4x4x32 slice. The times are simulated.
1024 devices in a mesh: ctx: 16 (over y, x), exp: 64 (over z, core).
Axes of the slice: x: 4, y: 4, z: 32, core: 2. Of those that a mesh axis runs over, the one named last changes fastest.
Arguments:
- queries: bfloat16 [64, 2048, 1536], P('exp', 'ctx'), may hold values from -6 to 6
- keys: bfloat16 [64, 2048, 1536], P('exp', 'ctx'), may hold values from -6 to 6
- values: bfloat16 [64, 2048, 1536], P('exp', 'ctx'), may hold values from -6 to 6
- log_decay: float32 [24, 64, 2048], P(None, 'exp', 'ctx'), may hold values from -0.9 to 0
- resid: bfloat16 [64, 2048, 1536], P('exp', 'ctx'), may hold values from -4 to 4
- gate_in: bfloat16 [64, 2048, 1536], P('exp', 'ctx'), may hold values from -8 to 8
- attn_gain: float32 [1536], replicated, may hold values from 0.5 to 1.5
- moe_gain: float32 [1536], replicated, may hold values from 0.5 to 1.5
- router_weight: bfloat16 [1536, 64], replicated, may hold values from -0.091796875 to 0.091796875
- expert_ids: int32 [64, 2048, 2], P('exp', 'ctx'), may hold values from 0 to 63, all different within a row; in each aligned block of 128 rows (0 to 127, 128 to 255, ..., all dimensions but the last counted through in order) at most 8 rows name the same one
- gate_weight: bfloat16 [64, 1536, 512], P('exp'), may hold values from -0.15625 to 0.15625
- up_weight: bfloat16 [64, 1536, 512], P('exp'), may hold values from -0.15625 to 0.15625
- down_weight: bfloat16 [64, 512, 1536], P('exp'), may hold values from -0.5 to 0.5
Outputs:
- layer_out: bfloat16 [64, 2048, 1536], P('exp', 'ctx')
Inputs may be any that keep to these rules, and one draw needn't show every extreme that they name: `expert_ids`: each token names 2 different experts. Among the 128 positions of one block of one document no expert is named more than 8 times, and in some blocks one is named exactly 8 times.
All inputs are finite; a program needn't handle non-finite values.
Results may differ from a plain program's by a relative error of at most 0.013.
Values may be sent and summed in bfloat16 or wider, within the bound.
No kernel may reach another device: no remote copies, remote signals or barrier semaphores. Data moves between devices by JAX's collectives and lax.ppermute only.
A program may use at most 64 MiB of HBM per device.

v0:
```python
import jax
import jax.numpy as jnp
from jax import lax
from jax.sharding import PartitionSpec as P

HIGHEST = lax.Precision.HIGHEST


def entering_2(value, axis, join, neutral):
    count, mine = (lax.axis_size(axis), lax.axis_index(axis))
    pieces = jax.tree.map(lambda part: lax.all_gather(part, axis), value)
    so_far = jax.tree.map(
        lambda part, zero: jnp.full_like(part, 0) + jnp.asarray(zero, part.dtype), value, neutral
    )

    def turn(position, so_far):
        longer = join(so_far, jax.tree.map(lambda part: part[position], pieces))
        return jax.tree.map(lambda new, old: jnp.where(position < mine, new, old), longer, so_far)

    return lax.fori_loop(0, count - 1, turn, so_far)


def combine_state(earlier, later):
    return (earlier[0] * later[0], later[0][:, None, None] * earlier[1] + later[1])


def apply_experts(arrived, gate_weight, up_weight, down_weight):
    exp_dev = gate_weight.shape[0]
    item_count = arrived.shape[1]
    features = arrived.shape[2]
    grouped = arrived.reshape(-1, exp_dev, item_count, features)
    gate_act = jnp.einsum(
        "send,edf->senf", grouped, gate_weight, preferred_element_type=jnp.float32
    )
    up_act = jnp.einsum("send,edf->senf", grouped, up_weight, preferred_element_type=jnp.float32)
    inner_act = (jax.nn.silu(gate_act) * up_act).astype(jnp.bfloat16)
    result = jnp.einsum(
        "senf,efd->send", inner_act, down_weight, preferred_element_type=jnp.float32
    )
    return result.astype(jnp.bfloat16).reshape(-1, item_count, features)


def on_device(
    queries,
    keys,
    values,
    log_decay,
    resid,
    gate_in,
    attn_gain,
    moe_gain,
    router_weight,
    expert_ids,
    gate_weight,
    up_weight,
    down_weight,
):
    tok_rows = queries.shape[1]
    features = queries.shape[2]
    head_count = log_decay.shape[0]
    head_size = features // head_count
    inv_root = head_size ** (-0.5)
    q_rows = queries.reshape(tok_rows, head_count, head_size)
    k_rows = keys.reshape(tok_rows, head_count, head_size)
    v_rows = values.reshape(tok_rows, head_count, head_size)
    decay_log = log_decay.reshape(head_count, tok_rows)
    cumulated = jnp.cumsum(decay_log, axis=1)
    positions = jnp.arange(tok_rows, dtype=jnp.int32)
    causal = (positions[:, None] >= positions[None, :])[None]
    gap_log = jnp.where(causal, cumulated[:, :, None] - cumulated[:, None, :], 0.0)
    damping = jnp.where(causal, jnp.exp(gap_log), 0.0)
    scores = (
        jnp.einsum("thd,shd->hts", q_rows, k_rows, preferred_element_type=jnp.float32)
        * inv_root
        * damping
    )
    scores = scores.astype(jnp.bfloat16)
    local_part = jnp.einsum("hts,shd->thd", scores, v_rows, preferred_element_type=jnp.float32)
    block_decay = jnp.exp(cumulated[:, -1])
    tail_decay = jnp.exp(cumulated[:, -1:] - cumulated)
    k_scaled = k_rows.astype(jnp.float32) * tail_decay.T[:, :, None]
    contribution = jnp.einsum(
        "thd,the->hde", k_scaled, v_rows.astype(jnp.float32), precision=HIGHEST
    )
    identity = (jnp.ones_like(block_decay), jnp.zeros_like(contribution))
    entering = entering_2((block_decay, contribution), "ctx", combine_state, identity)[1]
    carried = (
        jnp.einsum("thd,hde->the", q_rows.astype(jnp.float32), entering, precision=HIGHEST)
        * (inv_root * jnp.exp(cumulated)).T[:, :, None]
    )
    attention = local_part + carried
    mean_square = jnp.mean(attention * attention, axis=-1, keepdims=True)
    flat_resid = resid.reshape(tok_rows, features)
    normalized = (attention * lax.rsqrt(mean_square + 1e-05)).reshape(
        tok_rows, features
    ) * attn_gain
    flat_rows = (
        flat_resid.astype(jnp.float32)
        + normalized * jax.nn.sigmoid(gate_in.reshape(tok_rows, features).astype(jnp.float32))
    ).astype(jnp.bfloat16)
    h_float = flat_rows.astype(jnp.float32)
    moe_square = jnp.mean(h_float * h_float, axis=-1, keepdims=True)
    normed = (h_float * lax.rsqrt(moe_square + 1e-06) * moe_gain).astype(jnp.bfloat16)
    top_count = expert_ids.shape[2]
    chosen = expert_ids.reshape(tok_rows, top_count)
    experts = gate_weight.shape[0] * lax.axis_size("exp")
    capacity = 2 * top_count * tok_rows // experts
    affinity = jax.nn.sigmoid(jnp.dot(normed, router_weight, preferred_element_type=jnp.float32))
    labels = jnp.arange(experts, dtype=jnp.int32)
    picks = (chosen[:, :, None] == labels[None, None, :]).astype(jnp.float32)
    picked = jnp.sum(picks * affinity[:, None, :], axis=2)
    shares = picked / jnp.sum(picked, axis=1, keepdims=True)
    listed = chosen.reshape(-1)
    onehot = (listed[:, None] == labels[None, :]).astype(jnp.int32)
    before = jnp.cumsum(onehot, axis=0) - onehot
    slot_index = listed * capacity + jnp.sum(before * onehot, axis=1)
    slot_labels = jnp.arange(experts * capacity, dtype=jnp.int32)
    placing = jnp.sum(
        slot_labels[:, None, None] == slot_index.reshape(tok_rows, top_count)[None], axis=2
    ).astype(jnp.bfloat16)
    outgoing = (
        jnp.dot(placing, normed, preferred_element_type=jnp.float32)
        .astype(jnp.bfloat16)
        .reshape(experts, capacity, features)
    )
    arrived = lax.all_to_all(outgoing, "exp", split_axis=0, concat_axis=0, tiled=True)
    produced = apply_experts(arrived, gate_weight, up_weight, down_weight)
    returned = lax.all_to_all(produced, "exp", split_axis=0, concat_axis=0, tiled=True)
    gathered = jnp.take(returned.reshape(-1, features), slot_index, axis=0).reshape(
        tok_rows, top_count, features
    )
    mixture = jnp.sum(shares[:, :, None] * gathered.astype(jnp.float32), axis=1)
    return (h_float + mixture).astype(jnp.bfloat16).reshape(1, tok_rows, features)


def solution(mesh):
    placed = (
        P("exp", "ctx", None),
        P("exp", "ctx", None),
        P("exp", "ctx", None),
        P(None, "exp", "ctx"),
        P("exp", "ctx", None),
        P("exp", "ctx", None),
        P(),
        P(),
        P(),
        P("exp", "ctx", None),
        P("exp", None, None),
        P("exp", None, None),
        P("exp", None, None),
    )
    return jax.shard_map(
        on_device, mesh=mesh, in_specs=placed, out_specs=P("exp", "ctx", None), check_vma=False
    )
```

profile of v0, /device:TPU:6, one launch (start us, length us, event | category | flops | bytes accessed | tf_op | source)
XLA Modules:
  0.0 555.5 jit_solution(15501303174792217330)
XLA Ops:
  8.4 1.2 copy.64
  9.7 1.2 copy.65
  10.9 1.7 fusion.36
  13.6 1.3 dynamic-slice
  15.7 44.7 %all-reduce = f32[384]{0:T(512)S(1)} all-reduce(f32[384]{0:T(512)S(1)} %dynamic-update-slice), channel_id=2, replica_groups=mesh['ctx'=16,'exp'=64] {'ctx'}, use_global_device_ids=true, to_apply=%add | all-reduce | flops 384 | bytes 3072
  61.1 1.2 copy.63
  62.9 1.9 reduce-window.6
  64.9 1.6 slice_reduce_fusion
  68.9 1.5 broadcast_multiply_fusion.1
  70.4 1.4 copy.76
  72.5 1.4 convert_reduce_fusion
  73.9 72.0 %all-gather.4.cloned.1.call-done = f32[384,64,64]{2,1,0:T(8,128)} async-done(((f32[24,64,64]{2,1,0:T(8,128)}), f32[384,64,64]{2,1,0:T(8,128)}) %all-gather.4.cloned.1.call-update) | async-done | bytes 6291472 | tf_op jit(solution)/shard_map/all_gather | solution.py:11
  145.8 37.6 %while.14 = (s32[]{:T(128)}, f32[24,64,64]{2,1,0:T(8,128)S(1)}, s32[]{:T(128)}, f32[16,24]{1,0:T(8,128)}, f32[16,24,64,64]{3,2,1,0:T(8,128)}, /*index=5*/s32[]{:T(128)}, s32[]{:T(128)}) while((s32[]{:T(128)}, f32[24,64,64]{2,1,0:T(8,128)S(1)}, s32[]{:T(128)}, f32[16,24]{1,0:T(8,128)}, f32[16,24,64,64]{3,2,1,0:T(8,128)}, ...), condition=%wide.region_2.3_spmd.clone, body=%wide.region_1.2_spmd.clone.sunk | while | flops 393220 | bytes 1180041 | solution.py:20
  147.0 1.3 fusion.67
  149.5 1.3 fusion.67
  152.0 1.3 fusion.67
  154.5 1.3 fusion.67
  157.1 1.3 fusion.67
  159.6 1.3 fusion.67
  162.1 1.3 fusion.67
  164.6 1.3 fusion.67
  165.9 1.2 dynamic-slice_bitcast_fusion.2
  167.1 1.3 fusion.67
  168.4 1.2 dynamic-slice_bitcast_fusion.2
  169.6 1.3 fusion.67
  170.9 1.2 dynamic-slice_bitcast_fusion.2
  172.1 1.3 fusion.67
  173.4 1.2 dynamic-slice_bitcast_fusion.2
  174.6 1.3 fusion.67
  175.9 1.2 dynamic-slice_bitcast_fusion.2
  177.1 1.3 fusion.67
  179.6 1.3 fusion.67
  182.1 1.3 fusion.67
  183.4 2.4 fusion.17
  185.8 3.2 multiply_reduce_fusion.1
  189.0 1.2 broadcast_multiply_fusion
  190.6 1.5 fusion.32
  192.8 179.1 %all_to_all.10 = bf16[64,8,1536]{2,1,0:T(8,128)(2,1)S(1)} all-to-all(bf16[64,8,1536]{2,1,0:T(8,128)(2,1)S(1)} %fusion.1), channel_id=1, replica_groups=mesh['ctx'=16,'exp'=64] {'exp'}, dimensions={0} | all-to-all | bytes 3145728 | tf_op jit(solution)/shard_map/all_to_all | solution.py:126
  371.9 2.0 fusion.7
  373.8 4.7 convolution_convert_fusion
  378.5 5.0 all-to-all-start.1
  384.3 1.6 mul.198
  389.4 1.3 fusion.26
  392.1 2.3 copy.67
  394.4 144.6 %all-to-all-done.1 = bf16[64,8,1536]{2,1,0:T(8,128)(2,1)S(1)} async-done(((bf16[64,8,1536]{2,1,0:T(8,128)(2,1)}), bf16[64,8,1536]{2,1,0:T(8,128)(2,1)S(1)}, u32[]{:S(2)}, u32[]{:S(2)}) %all-to-all-start.1) | async-done | bytes 1572896 | tf_op jit(solution)/shard_map/all_to_all | solution.py:128
  539.0 2.3 gather_fusion
  541.3 2.3 gather.7
  543.5 4.0 multiply_reduce_fusion
  (72 shorter events, 27.1 us)
Async XLA Ops:
  6.5 367.3 %copy-start = (bf16[1,512,1536]{2,1,0:T(8,128)(2,1)S(1)}, bf16[1,512,1536]{2,1,0:T(8,128)(2,1)}, u32[]{:S(2)}) copy-start(bf16[1,512,1536]{2,1,0:T(8,128)(2,1)} %param.27) | copy-start | bytes 4718596
  6.5 139.3 %all-gather.4.cloned.1.call-start = ((), (), s32[]{:S(2)}) async-start(), calls=%async_computation.2 | async-start | bytes 13369344 | tf_op jit(solution)/shard_map/all_gather | solution.py:11
  9.7 3.0 copy-start.10
  12.7 48.3 %copy-start.6 = (s32[1,128,2]{2,1,0:T(8,128)}, s32[1,128,2]{2,1,0:T(8,128)S(1)}, u32[]{:S(2)}) copy-start(s32[1,128,2]{2,1,0:T(8,128)S(1)} %copy.70) | copy-start | bytes 3076
  68.1 315.4 %copy-start.9 = (s32[256]{0:T(256)}, s32[256]{0:T(256)S(1)}, u32[]{:S(2)}) copy-start(s32[256]{0:T(256)S(1)} %fusion.51) | copy-start | bytes 3076
  189.0 1.5 copy-start.7
  190.2 1.9 copy-start.1
  190.5 1.6 copy-start.5
  190.5 1.6 copy-start.12
  192.1 179.8 %copy-start.13 = (f32[128]{0:T(128)}, f32[128]{0:T(128)S(1)}, u32[]{:S(2)}) copy-start(f32[128]{0:T(128)S(1)} %add_rsqrt_fusion.1) | copy-start | bytes 1540
  192.8 179.1 %copy-start.14 = (bf16[1,1536,512]{2,1,0:T(8,128)(2,1)S(1)}, bf16[1,1536,512]{2,1,0:T(8,128)(2,1)}, u32[]{:S(2)}) copy-start(bf16[1,1536,512]{2,1,0:T(8,128)(2,1)} %param.25) | copy-start | bytes 4718596
  378.5 8.2 %copy-start.11 = (s32[1,128,2]{1,2,0:T(2,128)S(1)}, s32[1,128,2]{1,2,0:T(2,128)}, u32[]{:S(2)}) copy-start(s32[1,128,2]{1,2,0:T(2,128)} %param.24) | copy-start | bytes 3076
  378.5 160.4 %all-to-all-start.1 = ((bf16[64,8,1536]{2,1,0:T(8,128)(2,1)}), bf16[64,8,1536]{2,1,0:T(8,128)(2,1)S(1)}, u32[]{:S(2)}, u32[]{:S(2)}) async-start(bf16[64,8,1536]{2,1,0:T(8,128)(2,1)} %convolution_convert_fusion), calls=%async_computation.1 | async-start | bytes 3145728 | tf_op jit(solution)/shard_map/all_to_all | solution.py:128
  541.3 6.3 %copy-start.2 = (f32[1,128,1536]{2,1,0:T(8,128)S(1)}, f32[1,128,1536]{2,1,0:T(8,128)}, u32[]{:S(2)}) copy-start(f32[1,128,1536]{2,1,0:T(8,128)} %copy.67) | copy-start | bytes 2359300
  541.3 6.3 %copy-start.3 = (bf16[1,128,1536]{2,1,0:T(8,128)(2,1)S(1)}, bf16[1,128,1536]{2,1,0:T(8,128)(2,1)}, u32[]{:S(2)}) copy-start(bf16[1,128,1536]{2,1,0:T(8,128)(2,1)} %param.20) | copy-start | bytes 1179652
  543.5 4.0 copy-start.4
  543.5 4.0 copy-start.8
Sparse Core Ops, SparseCore 0:
  12.7 133.0 all-gather.3
where the time goes:
time: 557 us; the launch traced here: 555 us
  blocking collectives  224 us (40%)
  waiting for transfers between devices  217 us (39%)
  local copies, waits for them, and re-layouts  40.5 us (7%)
  other arithmetic  39.3 us (7%)
  matrix products  15.8 us (3%)
  between operations  14.3 us (3%)
    all_to_all x1, blocking collectives, on_device(): lax.all_to_all(outgoing, 'exp', split_axis=0, concat_axis=0, tiled=True)  179 us
    all_to_all x1, waiting for transfers between devices, on_device(): lax.all_to_all(produced, 'exp', split_axis=0, concat_axis=0, tiled=True)  145 us
    all_gather x1, waiting for transfers between devices, entering_2(): pieces = jax.tree.map(lambda part: lax.all_gather(part, axis), value)  72 us
    unnamed x1, blocking collectives  44.7 us
    select_n x15, other arithmetic, turn(): jnp.where(position < mine, new, old)  19.5 us
    mul x15, local copies, waits for them, and re-layouts, combine_state(): later[0][:, None, None] * earlier[1] + later[1]  17.8 us
  transfers between devices with their start and end apart: 2, of which 2 were waited for; matrix products, arithmetic and copies ran while one was open for 5% of the time, Pallas kernels for 0%

commit v1 on v0

--- a/solution.py
+++ b/solution.py
@@ -6,18 +6,22 @@
 HIGHEST = lax.Precision.HIGHEST
 
 
-def entering_2(value, axis, join, neutral):
+def entering_scan(block_decay, contribution, axis):
     count, mine = (lax.axis_size(axis), lax.axis_index(axis))
-    pieces = jax.tree.map(lambda part: lax.all_gather(part, axis), value)
-    so_far = jax.tree.map(
-        lambda part, zero: jnp.full_like(part, 0) + jnp.asarray(zero, part.dtype), value, neutral
-    )
-
-    def turn(position, so_far):
-        longer = join(so_far, jax.tree.map(lambda part: part[position], pieces))
-        return jax.tree.map(lambda new, old: jnp.where(position < mine, new, old), longer, so_far)
-
-    return lax.fori_loop(0, count - 1, turn, so_far)
+    shift_pairs = [(i, i + 1) for i in range(count - 1)]
+    decay = lax.ppermute(block_decay, axis, shift_pairs)
+    state = lax.ppermute(contribution, axis, shift_pairs)
+    decay = jnp.where(mine == 0, jnp.ones_like(decay), decay)
+    step = 1
+    while step < count - 1:
+        pairs = [(i, i + step) for i in range(count - step)]
+        got_decay = lax.ppermute(decay, axis, pairs)
+        got_state = lax.ppermute(state, axis, pairs)
+        has = mine >= step
+        state = jnp.where(has, decay[:, None, None] * got_state + state, state)
+        decay = jnp.where(has, got_decay * decay, decay)
+        step *= 2
+    return state
 
 
 def combine_state(earlier, later):
@@ -82,8 +86,7 @@
     contribution = jnp.einsum(
         "thd,the->hde", k_scaled, v_rows.astype(jnp.float32), precision=HIGHEST
     )
-    identity = (jnp.ones_like(block_decay), jnp.zeros_like(contribution))
-    entering = entering_2((block_decay, contribution), "ctx", combine_state, identity)[1]
+    entering = entering_scan(block_decay, contribution, "ctx")
     carried = (
         jnp.einsum("thd,hde->the", q_rows.astype(jnp.float32), entering, precision=HIGHEST)
         * (inv_root * jnp.exp(cumulated)).T[:, :, None]

time: 557 us -> 485 us (0.87)
  blocking collectives: 224 us -> 185 us
  starting transfers between devices: 4.99 us -> 40.6 us
  local copies, waits for them, and re-layouts: 40.5 us -> 19.4 us
  other arithmetic: 39.3 us -> 21 us
  waiting for transfers between devices: 217 us -> 200 us
  between operations: 14.3 us -> 0.42 us
    all_gather x1 -> x0, waiting for transfers between devices: 72 us -> none  [entering_2(): pieces = jax.tree.map(lambda part: lax.all_gather(part, axis), value)]
    ppermute x0 -> x9, waiting for transfers between devices: none -> 55.7 us  [the longest x3 23.8 us: entering_scan(): got_decay = lax.ppermute(decay, axis, pairs)]
    unnamed x1 -> x0, blocking collectives: 44.7 us -> none
    ppermute x0 -> x9, starting transfers between devices: none -> 35.6 us  [the longest x4 19.9 us: entering_scan(): got_state = lax.ppermute(state, axis, pairs)]
    mul x15 -> x0, local copies, waits for them, and re-layouts: 17.8 us -> none  [combine_state(): later[0][:, None, None] * earlier[1] + later[1]]
    select_n x15 -> x7, other arithmetic: 19.5 us -> 5.48 us  [the longest x3 4.1 us: entering_scan(): state = jnp.where(has, decay[:, None, None] * got_state + state, state)]
    all_to_all x1, blocking collectives: 179 us -> 185 us  [on_device(): lax.all_to_all(outgoing, 'exp', split_axis=0, concat_axis=0, tiled=True)]
  transfers between devices with their start and end apart: 2 -> 10, of which waited for: 2 -> 7; matrix products, arithmetic and copies ran while one was open for 5% -> 5% of each run, Pallas kernels for 0% -> 0%
where the time goes in v1:
time: 485 us; the launch traced here: 481 us
  waiting for transfers between devices  200 us (41%)
  blocking collectives  185 us (38%)
  starting transfers between devices  40.6 us (8%)
  other arithmetic  21 us (4%)
  local copies, waits for them, and re-layouts  19.4 us (4%)
  matrix products  14.3 us (3%)
    all_to_all x1, blocking collectives, on_device(): lax.all_to_all(outgoing, 'exp', split_axis=0, concat_axis=0, tiled=True)  185 us
    all_to_all x1, waiting for transfers between devices, on_device(): lax.all_to_all(produced, 'exp', split_axis=0, concat_axis=0, tiled=True)  145 us
    ppermute x3, waiting for transfers between devices, entering_scan(): got_decay = lax.ppermute(decay, axis, pairs)  23.8 us
    ppermute x4, starting transfers between devices, entering_scan(): got_state = lax.ppermute(state, axis, pairs)  19.9 us
    ppermute x4, waiting for transfers between devices, entering_scan(): got_state = lax.ppermute(state, axis, pairs)  17.6 us
    ppermute x1, waiting for transfers between devices, entering_scan(): state = lax.ppermute(contribution, axis, shift_pairs)  14.3 us
  transfers between devices with their start and end apart: 10, of which 7 were waited for; matrix products, arithmetic and copies ran while one was open for 5% of the time, Pallas kernels for 0%

profile of v1, /device:TPU:6, one launch (start us, length us, event | category | flops | bytes accessed | tf_op | source)
XLA Modules:
  0.0 480.8 jit_solution(1963531566627390748)
XLA Ops:
  0.0 1.1 reduce_window_sum.26
  1.4 1.3 copy.52
  2.7 1.2 copy.53
  3.9 1.6 fusion.36
  5.5 3.4 collective-permute-start.4
  8.9 3.4 collective-permute-start
  12.7 14.3 %collective-permute-done.4 = f32[24,64,64]{2,1,0:T(8,128)} collective-permute-done((f32[24,64,64]{2,1,0:T(8,128)}, f32[24,64,64]{2,1,0:T(8,128)}, u32[]{:S(2)}, u32[]{:S(2)}) %collective-permute-start.4) | collective-permute-done | bytes 393248 | tf_op jit(solution)/shard_map/ppermute | solution.py:13
  27.0 5.5 %collective-permute-start.5 = (f32[24,64,64]{2,1,0:T(8,128)}, f32[24,64,64]{2,1,0:T(8,128)}, u32[]{:S(2)}, u32[]{:S(2)}) collective-permute-start(f32[24,64,64]{2,1,0:T(8,128)} %collective-permute-done.4), channel_id=1, source_target_pairs={{0,64},{64,128},{128,192},{192,256},{256,320},{320,384},{384,448},... | collective-permute-start | bytes 1179656 | tf_op jit(solution)/shard_map/ppermute | solution.py:19
  32.5 2.0 convolution_bitcast_fusion.1
  34.7 14.0 %collective-permute-done.5 = f32[24,64,64]{2,1,0:T(8,128)} collective-permute-done((f32[24,64,64]{2,1,0:T(8,128)}, f32[24,64,64]{2,1,0:T(8,128)}, u32[]{:S(2)}, u32[]{:S(2)}) %collective-permute-start.5) | collective-permute-done | bytes 393248 | tf_op jit(solution)/shard_map/ppermute | solution.py:19
  48.7 1.5 add_select_fusion.3
  50.3 4.1 collective-permute-start.6
  54.4 4.3 collective-permute-start.1
  58.7 1.2 reduce-window.6
  60.0 13.2 %collective-permute-done.1 = f32[24]{0:T(128)S(1)} collective-permute-done((f32[24]{0:T(128)S(1)}, f32[24]{0:T(128)S(1)}, u32[]{:S(2)}, u32[]{:S(2)}) %collective-permute-start.1) | collective-permute-done | bytes 128 | tf_op jit(solution)/shard_map/ppermute | solution.py:18
  73.2 1.3 add_select_fusion.2
  74.5 4.4 collective-permute-start.7
  79.1 1.0 reshape_reshape.3
  80.1 0.9 fusion.53
  81.0 2.6 collective-permute-start.2
  83.6 0.8 reduce_sum.77
  84.4 3.7 collective-permute-done.2
  88.7 3.5 collective-permute-done.7
  92.3 1.3 add_select_fusion.1
  93.6 5.9 %collective-permute-start.8 = (f32[24,64,64]{2,1,0:T(8,128)S(1)}, f32[24,64,64]{2,1,0:T(8,128)S(1)}, u32[]{:S(2)}, u32[]{:S(2)}) collective-permute-start(f32[24,64,64]{2,1,0:T(8,128)S(1)} %add_select_fusion.1), channel_id=1, source_target_pairs={{0,512},{64,576},{128,640},{192,704},{256,768},{320,832},{384,896}... | collective-permute-start | bytes 1179656 | tf_op jit(solution)/shard_map/ppermute | solution.py:19
  99.5 1.5 broadcast_multiply_fusion.1
  101.0 1.5 copy.64
  102.5 1.5 convert_reduce_fusion
  103.9 2.1 collective-permute-start.3
  106.0 6.9 %collective-permute-done.3 = f32[24]{0:T(128)} collective-permute-done((f32[24]{0:T(128)}, f32[24]{0:T(128)}, u32[]{:S(2)}, u32[]{:S(2)}) %collective-permute-start.3) | collective-permute-done | bytes 128 | tf_op jit(solution)/shard_map/ppermute | solution.py:18
  113.6 2.0 multiply_reduce_fusion.1
  116.3 1.5 fusion.31
  119.2 184.9 %all_to_all.10 = bf16[64,8,1536]{2,1,0:T(8,128)(2,1)S(1)} all-to-all(bf16[64,8,1536]{2,1,0:T(8,128)(2,1)S(1)} %fusion), channel_id=1, replica_groups=mesh['ctx'=16,'exp'=64] {'exp'}, dimensions={0} | all-to-all | bytes 3145728 | tf_op jit(solution)/shard_map/all_to_all | solution.py:129
  304.1 2.0 fusion.6
  306.0 4.7 convolution_convert_fusion
  310.7 5.0 %all-to-all-start.1 = ((bf16[64,8,1536]{2,1,0:T(8,128)(2,1)}), bf16[64,8,1536]{2,1,0:T(8,128)(2,1)S(1)}, u32[]{:S(2)}, u32[]{:S(2)}) async-start(bf16[64,8,1536]{2,1,0:T(8,128)(2,1)} %convolution_convert_fusion), calls=%async_computation.1 | async-start | bytes 3145728 | tf_op jit(solution)/shard_map/all_to_all | solution.py:131
  315.7 0.8 reduce_sum.76
  316.5 1.6 mul.226
  318.0 0.9 copy.61
  319.5 0.8 copy.62
  321.6 2.3 copy.55
  323.9 1.3 fusion.25
  325.9 0.7 copy.57
  326.6 144.5 %all-to-all-done.1 = bf16[64,8,1536]{2,1,0:T(8,128)(2,1)S(1)} async-done(((bf16[64,8,1536]{2,1,0:T(8,128)(2,1)}), bf16[64,8,1536]{2,1,0:T(8,128)(2,1)S(1)}, u32[]{:S(2)}, u32[]{:S(2)}) %all-to-all-start.1) | async-done | bytes 1572896 | tf_op jit(solution)/shard_map/all_to_all | solution.py:131
  471.2 2.3 gather_fusion
  473.4 2.3 gather.7
  475.7 4.0 multiply_reduce_fusion
  479.8 1.0 fusion.34
  (68 shorter events, 6.9 us)
Async XLA Ops:
  0.0 306.0 %copy-start = (bf16[1,512,1536]{2,1,0:T(8,128)(2,1)S(1)}, bf16[1,512,1536]{2,1,0:T(8,128)(2,1)}, u32[]{:S(2)}) copy-start(bf16[1,512,1536]{2,1,0:T(8,128)(2,1)} %param.25) | copy-start | bytes 4718596
  1.4 11.0 %copy-start.13 = (s32[1,128,2]{1,2,0:T(2,128)S(1)}, s32[1,128,2]{1,2,0:T(2,128)}, u32[]{:S(2)}) copy-start(s32[1,128,2]{1,2,0:T(2,128)} %param.22) | copy-start | bytes 3076
  1.4 11.1 %copy-start.8 = (bf16[1,128,1536]{2,1,0:T(8,128)(2,1)S(1)}, bf16[1,128,1536]{2,1,0:T(8,128)(2,1)}, u32[]{:S(2)}) copy-start(bf16[1,128,1536]{2,1,0:T(8,128)(2,1)} %param.13) | copy-start | bytes 1179652
  5.5 21.5 %collective-permute-start.4 = (f32[24,64,64]{2,1,0:T(8,128)}, f32[24,64,64]{2,1,0:T(8,128)}, u32[]{:S(2)}, u32[]{:S(2)}) collective-permute-start(f32[24,64,64]{2,1,0:T(8,128)} %fusion.36), channel_id=1, source_target_pairs={{0,64},{64,128},{128,192},{192,256},{256,320},{320,384},{384,448},... | collective-permute-start | bytes 1179656 | tf_op jit(solution)/shard_map/ppermute | solution.py:13
  8.9 25.8 %collective-permute-start = (f32[24]{0:T(128)S(1)}, f32[24]{0:T(128)S(1)}, u32[]{:S(2)}, u32[]{:S(2)}) collective-permute-start(f32[24]{0:T(128)S(1)} %exp.31), channel_id=1, source_target_pairs={{0,64},{64,128},{128,192},{192,256},{256,320},{320,384},{384,448},... | collective-permute-start | bytes 296 | tf_op jit(solution)/shard_map/ppermute | solution.py:12
  12.5 22.1 %copy-start.6 = (s32[1,128,2]{2,1,0:T(8,128)}, s32[1,128,2]{2,1,0:T(8,128)S(1)}, u32[]{:S(2)}) copy-start(s32[1,128,2]{2,1,0:T(8,128)S(1)} %copy.58) | copy-start | bytes 3076
  27.0 21.7 %collective-permute-start.5 = (f32[24,64,64]{2,1,0:T(8,128)}, f32[24,64,64]{2,1,0:T(8,128)}, u32[]{:S(2)}, u32[]{:S(2)}) collective-permute-start(f32[24,64,64]{2,1,0:T(8,128)} %collective-permute-done.4), channel_id=1, source_target_pairs={{0,64},{64,128},{128,192},{192,256},{256,320},{320,384},{384,448},... | collective-permute-start | bytes 1179656 | tf_op jit(solution)/shard_map/ppermute | solution.py:19
  50.3 22.9 %collective-permute-start.6 = (f32[24,64,64]{2,1,0:T(8,128)S(1)}, f32[24,64,64]{2,1,0:T(8,128)}, u32[]{:S(2)}, u32[]{:S(2)}) collective-permute-start(f32[24,64,64]{2,1,0:T(8,128)S(1)} %add_select_fusion.3), channel_id=1, source_target_pairs={{0,128},{64,192},{128,256},{192,320},{256,384},{320,448},{384,512}... | collective-permute-start | bytes 1179656 | tf_op jit(solution)/shard_map/ppermute | solution.py:19
  54.4 18.7 %collective-permute-start.1 = (f32[24]{0:T(128)S(1)}, f32[24]{0:T(128)S(1)}, u32[]{:S(2)}, u32[]{:S(2)}) collective-permute-start(f32[24]{0:T(128)S(1)} %broadcast_select_fusion.1), channel_id=1, source_target_pairs={{0,64},{64,128},{128,192},{192,256},{256,320},{320,384},{384,448},... | collective-permute-start | bytes 296 | tf_op jit(solution)/shard_map/ppermute | solution.py:18
  60.0 18.9 %copy-start.7 = (s32[64,2,128]{2,0,1:T(8,128)S(1)}, s32[64,2,128]{2,0,1:T(8,128)}, u32[]{:S(2)}) copy-start(s32[64,2,128]{2,0,1:T(8,128)} %reduce-window.6) | copy-start | bytes 196612
  73.2 1.3 copy-start.16
  74.5 17.8 %collective-permute-start.7 = (f32[24,64,64]{2,1,0:T(8,128)S(1)}, f32[24,64,64]{2,1,0:T(8,128)}, u32[]{:S(2)}, u32[]{:S(2)}) collective-permute-start(f32[24,64,64]{2,1,0:T(8,128)S(1)} %add_select_fusion.2), channel_id=1, source_target_pairs={{0,256},{64,320},{128,384},{192,448},{256,512},{320,576},{384,640}... | collective-permute-start | bytes 1179656 | tf_op jit(solution)/shard_map/ppermute | solution.py:19
  81.0 234.7 %copy-start.12 = (s32[256]{0:T(256)}, s32[256]{0:T(256)S(1)}, u32[]{:S(2)}) copy-start(s32[256]{0:T(256)S(1)} %fusion.53) | copy-start | bytes 3076
  81.0 7.0 %collective-permute-start.2 = (f32[24]{0:T(128)}, f32[24]{0:T(128)S(1)}, u32[]{:S(2)}, u32[]{:S(2)}) collective-permute-start(f32[24]{0:T(128)} %copy-done.16), channel_id=1, source_target_pairs={{0,128},{64,192},{128,256},{192,320},{256,384},{320,448},{384,512}... | collective-permute-start | bytes 296 | tf_op jit(solution)/shard_map/ppermute | solution.py:18
  84.4 15.1 %copy-start.9 = (s32[1,128,2]{2,1,0:T(8,128)S(1)}, s32[1,128,2]{2,1,0:T(8,128)}, u32[]{:S(2)}) copy-start(s32[1,128,2]{2,1,0:T(8,128)} %reduce_sum.77) | copy-start | bytes 3076
  88.7 12.2 %copy-start.17 = (f32[24]{0:T(128)}, f32[24]{0:T(128)S(1)}, u32[]{:S(2)}) copy-start(f32[24]{0:T(128)S(1)} %broadcast_select_fusion.3) | copy-start | bytes 292
  93.6 20.0 %collective-permute-start.8 = (f32[24,64,64]{2,1,0:T(8,128)S(1)}, f32[24,64,64]{2,1,0:T(8,128)S(1)}, u32[]{:S(2)}, u32[]{:S(2)}) collective-permute-start(f32[24,64,64]{2,1,0:T(8,128)S(1)} %add_select_fusion.1), channel_id=1, source_target_pairs={{0,512},{64,576},{128,640},{192,704},{256,768},{320,832},{384,896}... | collective-permute-start | bytes 1179656 | tf_op jit(solution)/shard_map/ppermute | solution.py:19
  103.9 9.0 %collective-permute-start.3 = (f32[24]{0:T(128)}, f32[24]{0:T(128)}, u32[]{:S(2)}, u32[]{:S(2)}) collective-permute-start(f32[24]{0:T(128)} %copy-done.17), channel_id=1, source_target_pairs={{0,256},{64,320},{128,384},{192,448},{256,512},{320,576},{384,640}... | collective-permute-start | bytes 296 | tf_op jit(solution)/shard_map/ppermute | solution.py:18
  115.6 0.7 copy-start.10
  115.7 2.1 copy-start.1
  116.3 2.1 copy-start.5
  116.3 2.1 copy-start.15
  117.9 0.6 copy-start.18
  119.1 184.9 %copy-start.19 = (bf16[1,1536,512]{2,1,0:T(8,128)(2,1)S(1)}, bf16[1,1536,512]{2,1,0:T(8,128)(2,1)}, u32[]{:S(2)}) copy-start(bf16[1,1536,512]{2,1,0:T(8,128)(2,1)} %param.23) | copy-start | bytes 4718596
  310.7 8.2 %copy-start.14 = (s32[1,128,2]{1,2,0:T(2,128)S(1)}, s32[1,128,2]{1,2,0:T(2,128)}, u32[]{:S(2)}) copy-start(s32[1,128,2]{1,2,0:T(2,128)} %param.22) | copy-start | bytes 3076
  310.7 160.4 %all-to-all-start.1 = ((bf16[64,8,1536]{2,1,0:T(8,128)(2,1)}), bf16[64,8,1536]{2,1,0:T(8,128)(2,1)S(1)}, u32[]{:S(2)}, u32[]{:S(2)}) async-start(bf16[64,8,1536]{2,1,0:T(8,128)(2,1)} %convolution_convert_fusion), calls=%async_computation.1 | async-start | bytes 3145728 | tf_op jit(solution)/shard_map/all_to_all | solution.py:131
  473.4 6.3 %copy-start.2 = (f32[1,128,1536]{2,1,0:T(8,128)S(1)}, f32[1,128,1536]{2,1,0:T(8,128)}, u32[]{:S(2)}) copy-start(f32[1,128,1536]{2,1,0:T(8,128)} %copy.55) | copy-start | bytes 2359300
  473.4 6.3 %copy-start.3 = (bf16[1,128,1536]{2,1,0:T(8,128)(2,1)S(1)}, bf16[1,128,1536]{2,1,0:T(8,128)(2,1)}, u32[]{:S(2)}) copy-start(bf16[1,128,1536]{2,1,0:T(8,128)(2,1)} %param.18) | copy-start | bytes 1179652
  475.7 4.0 copy-start.4
  475.7 4.0 copy-start.11

commit v2 on v1

--- a/solution.py
+++ b/solution.py
@@ -8,15 +8,27 @@
 
 def entering_scan(block_decay, contribution, axis):
     count, mine = (lax.axis_size(axis), lax.axis_index(axis))
-    shift_pairs = [(i, i + 1) for i in range(count - 1)]
-    decay = lax.ppermute(block_decay, axis, shift_pairs)
-    state = lax.ppermute(contribution, axis, shift_pairs)
+    rows = contribution.shape[1]
+    decay_row = jnp.broadcast_to(block_decay[:, None, None], contribution.shape[:1] + (1,) + contribution.shape[2:])
+    packed = jnp.concatenate([contribution, decay_row], axis=1)
+
+    def split(value):
+        return value[:, :rows], value[:, rows, 0]
+
+    def shifted(value, step):
+        return lax.ppermute(value, axis, [(i, i + step) for i in range(count - step)])
+
+    state, decay = split(shifted(packed, 1))
     decay = jnp.where(mine == 0, jnp.ones_like(decay), decay)
     step = 1
+    if count > 2:
+        older_state, older_decay = split(shifted(packed, 2))
+        has = mine >= 2
+        state = jnp.where(has, decay[:, None, None] * older_state + state, state)
+        decay = jnp.where(has, older_decay * decay, decay)
+        step = 2
     while step < count - 1:
-        pairs = [(i, i + step) for i in range(count - step)]
-        got_decay = lax.ppermute(decay, axis, pairs)
-        got_state = lax.ppermute(state, axis, pairs)
+        got_state, got_decay = split(shifted(jnp.concatenate([state, jnp.broadcast_to(decay[:, None, None], decay_row.shape)], axis=1), step))
         has = mine >= step
         state = jnp.where(has, decay[:, None, None] * got_state + state, state)
         decay = jnp.where(has, got_decay * decay, decay)

time: 485 us -> 501 us (1.033)
  other arithmetic: 21 us -> 34.2 us
  starting transfers between devices: 40.6 us -> 28.8 us
  waiting for transfers between devices: 200 us -> 207 us
    ppermute x9 -> x5, starting transfers between devices: 35.6 us -> 23.8 us  [shifted(): lax.ppermute(value, axis, [(i, i + step) for i in range(count - step)])]
    ppermute x9 -> x5, waiting for transfers between devices: 55.7 us -> 62.6 us  [shifted(): lax.ppermute(value, axis, [(i, i + step) for i in range(count - step)])]
  transfers between devices with their start and end apart: 10 -> 6, of which waited for: 7 -> 6; matrix products, arithmetic and copies ran while one was open for 5% -> 5% of each run, Pallas kernels for 0% -> 0%
where the time goes in v2:
time: 501 us; the launch traced here: 492 us
  waiting for transfers between devices  207 us (41%)
  blocking collectives  185 us (37%)
  other arithmetic  34.2 us (7%)
  starting transfers between devices  28.8 us (6%)
  local copies, waits for them, and re-layouts  21.9 us (4%)
  matrix products  14.9 us (3%)
    all_to_all x1, blocking collectives, on_device(): lax.all_to_all(outgoing, 'exp', split_axis=0, concat_axis=0, tiled=True)  185 us
    all_to_all x1, waiting for transfers between devices, on_device(): lax.all_to_all(produced, 'exp', split_axis=0, concat_axis=0, tiled=True)  145 us
    ppermute x5, waiting for transfers between devices, shifted(): lax.ppermute(value, axis, [(i, i + step) for i in range(count - step)])  62.6 us
    ppermute x5, starting transfers between devices, shifted(): lax.ppermute(value, axis, [(i, i + step) for i in range(count - step)])  23.8 us
  transfers between devices with their start and end apart: 6, of which 6 were waited for; matrix products, arithmetic and copies ran while one was open for 5% of the time, Pallas kernels for 0%

profile of v2, /device:TPU:6, one launch (start us, length us, event | category | flops | bytes accessed | tf_op | source)
XLA Modules:
  0.0 492.5 jit_solution(10168195095080317778)
XLA Ops:
  0.0 1.1 reduce_window_sum.26
  1.9 1.2 copy.49
  3.2 1.4 copy.50
  4.5 0.8 fusion.35
  5.4 1.2 pad_maximum_fusion
  6.6 4.3 collective-permute-start
  10.9 4.0 collective-permute-start.1
  15.0 14.5 %collective-permute-done = f32[24,65,64]{1,2,0:T(8,128)S(1)} collective-permute-done((f32[24,65,64]{1,2,0:T(8,128)}, f32[24,65,64]{1,2,0:T(8,128)S(1)}, u32[]{:S(2)}, u32[]{:S(2)}) %collective-permute-start) | collective-permute-done | bytes 399392 | tf_op jit(solution)/shard_map/ppermute | solution.py:19
  29.9 15.3 %collective-permute-done.1 = f32[24,65,64]{1,2,0:T(8,128)S(1)} collective-permute-done((f32[24,65,64]{1,2,0:T(8,128)}, f32[24,65,64]{1,2,0:T(8,128)S(1)}, u32[]{:S(2)}, u32[]{:S(2)}) %collective-permute-start.1) | collective-permute-done | bytes 399392 | tf_op jit(solution)/shard_map/ppermute | solution.py:19
  45.6 1.3 add_select_fusion.3
  47.1 1.2 pad_maximum_fusion.1
  48.2 5.5 %collective-permute-start.2 = (f32[24,65,64]{1,2,0:T(8,128)}, f32[24,65,64]{1,2,0:T(8,128)S(1)}, u32[]{:S(2)}, u32[]{:S(2)}) collective-permute-start(f32[24,65,64]{1,2,0:T(8,128)} %pad_maximum_fusion.1), channel_id=1, source_target_pairs={{0,128},{64,192},{128,256},{192,320},{256,384},{320,448},{384,512}... | collective-permute-start | bytes 1198088 | tf_op jit(solution)/shard_map/ppermute | solution.py:19
  54.7 1.2 copy.48
  55.9 14.4 %collective-permute-done.2 = f32[24,65,64]{1,2,0:T(8,128)S(1)} collective-permute-done((f32[24,65,64]{1,2,0:T(8,128)}, f32[24,65,64]{1,2,0:T(8,128)S(1)}, u32[]{:S(2)}, u32[]{:S(2)}) %collective-permute-start.2) | collective-permute-done | bytes 399392 | tf_op jit(solution)/shard_map/ppermute | solution.py:19
  70.3 2.9 fusion.60
  73.2 1.6 reduce.2
  74.8 1.3 add_select_fusion.2
  76.2 1.2 pad_maximum_fusion.2
  77.3 3.5 collective-permute-start.3
  81.5 1.9 reduce-window.6
  83.4 1.6 slice_reduce_fusion
  85.7 0.9 fusion.52
  87.4 8.9 %collective-permute-done.3 = f32[24,65,64]{1,2,0:T(8,128)S(1)} collective-permute-done((f32[24,65,64]{1,2,0:T(8,128)}, f32[24,65,64]{1,2,0:T(8,128)S(1)}, u32[]{:S(2)}, u32[]{:S(2)}) %collective-permute-start.3) | collective-permute-done | bytes 399392 | tf_op jit(solution)/shard_map/ppermute | solution.py:19
  96.3 1.6 fusion.54
  98.6 1.3 add_select_fusion.1
  100.0 1.2 pad_maximum_fusion.3
  101.2 6.5 %collective-permute-start.4 = (f32[24,65,64]{1,2,0:T(8,128)}, f32[24,65,64]{1,2,0:T(8,128)}, u32[]{:S(2)}, u32[]{:S(2)}) collective-permute-start(f32[24,65,64]{1,2,0:T(8,128)} %pad_maximum_fusion.3), channel_id=1, source_target_pairs={{0,512},{64,576},{128,640},{192,704},{256,768},{320,832},{384,896}... | collective-permute-start | bytes 1198088 | tf_op jit(solution)/shard_map/ppermute | solution.py:19
  108.3 1.6 copy.60
  110.5 1.5 convert_reduce_fusion
  112.0 9.4 %collective-permute-done.4 = f32[24,65,64]{1,2,0:T(8,128)} collective-permute-done((f32[24,65,64]{1,2,0:T(8,128)}, f32[24,65,64]{1,2,0:T(8,128)}, u32[]{:S(2)}, u32[]{:S(2)}) %collective-permute-start.4) | collective-permute-done | bytes 399392 | tf_op jit(solution)/shard_map/ppermute | solution.py:19
  121.4 2.7 fusion.16
  124.1 2.9 multiply_reduce_fusion.1
  128.4 1.5 fusion.31
  130.7 184.9 %all_to_all.10 = bf16[64,8,1536]{2,1,0:T(8,128)(2,1)S(1)} all-to-all(bf16[64,8,1536]{2,1,0:T(8,128)(2,1)S(1)} %fusion), channel_id=1, replica_groups=mesh['ctx'=16,'exp'=64] {'exp'}, dimensions={0} | all-to-all | bytes 3145728 | tf_op jit(solution)/shard_map/all_to_all | solution.py:141
  315.6 2.0 fusion.6
  317.5 4.7 convolution_convert_fusion
  322.2 5.0 %all-to-all-start.1 = ((bf16[64,8,1536]{2,1,0:T(8,128)(2,1)}), bf16[64,8,1536]{2,1,0:T(8,128)(2,1)S(1)}, u32[]{:S(2)}, u32[]{:S(2)}) async-start(bf16[64,8,1536]{2,1,0:T(8,128)(2,1)} %convolution_convert_fusion), calls=%async_computation.1 | async-start | bytes 3145728 | tf_op jit(solution)/shard_map/all_to_all | solution.py:143
  327.2 0.8 reduce_sum.76
  328.0 1.6 mul.250
  329.6 0.9 copy.57
  331.0 0.8 copy.58
  333.1 1.3 fusion.25
  335.8 2.3 copy.51
  338.1 144.7 %all-to-all-done.1 = bf16[64,8,1536]{2,1,0:T(8,128)(2,1)S(1)} async-done(((bf16[64,8,1536]{2,1,0:T(8,128)(2,1)}), bf16[64,8,1536]{2,1,0:T(8,128)(2,1)S(1)}, u32[]{:S(2)}, u32[]{:S(2)}) %all-to-all-start.1) | async-done | bytes 1572896 | tf_op jit(solution)/shard_map/all_to_all | solution.py:143
  482.9 2.3 gather_fusion
  485.1 2.3 gather.7
  487.4 4.0 multiply_reduce_fusion
  491.5 1.0 fusion.34
  (85 shorter events, 12.4 us)
Async XLA Ops:
  0.0 317.5 %copy-start = (bf16[1,512,1536]{2,1,0:T(8,128)(2,1)S(1)}, bf16[1,512,1536]{2,1,0:T(8,128)(2,1)}, u32[]{:S(2)}) copy-start(bf16[1,512,1536]{2,1,0:T(8,128)(2,1)} %param.25) | copy-start | bytes 4718596
  3.1 2.3 copy-start.3
  4.5 2.1 copy-start.5
  6.6 22.9 %collective-permute-start = (f32[24,65,64]{1,2,0:T(8,128)}, f32[24,65,64]{1,2,0:T(8,128)S(1)}, u32[]{:S(2)}, u32[]{:S(2)}) collective-permute-start(f32[24,65,64]{1,2,0:T(8,128)} %pad_maximum_fusion), channel_id=1, source_target_pairs={{0,128},{64,192},{128,256},{192,320},{256,384},{320,448},{384,512}... | collective-permute-start | bytes 1198088 | tf_op jit(solution)/shard_map/ppermute | solution.py:19
  10.9 34.3 %collective-permute-start.1 = (f32[24,65,64]{1,2,0:T(8,128)}, f32[24,65,64]{1,2,0:T(8,128)S(1)}, u32[]{:S(2)}, u32[]{:S(2)}) collective-permute-start(f32[24,65,64]{1,2,0:T(8,128)} %pad_maximum_fusion), channel_id=1, source_target_pairs={{0,64},{64,128},{128,192},{192,256},{256,320},{320,384},{384,448},... | collective-permute-start | bytes 1198088 | tf_op jit(solution)/shard_map/ppermute | solution.py:19
  29.5 16.1 %copy-start.12 = (f32[24,65,64]{1,2,0:T(8,128)}, f32[24,65,64]{1,2,0:T(8,128)S(1)}, u32[]{:S(2)}) copy-start(f32[24,65,64]{1,2,0:T(8,128)S(1)} %collective-permute-done) | copy-start | bytes 1198084
  45.2 1.8 copy-start.13
  45.6 1.5 copy-start.23
  46.9 6.9 %copy-start.20 = (s32[1,128,2]{1,2,0:T(2,128)S(1)}, s32[1,128,2]{1,2,0:T(2,128)}, u32[]{:S(2)}) copy-start(s32[1,128,2]{1,2,0:T(2,128)} %param.22) | copy-start | bytes 3076
  48.2 22.1 %collective-permute-start.2 = (f32[24,65,64]{1,2,0:T(8,128)}, f32[24,65,64]{1,2,0:T(8,128)S(1)}, u32[]{:S(2)}, u32[]{:S(2)}) collective-permute-start(f32[24,65,64]{1,2,0:T(8,128)} %pad_maximum_fusion.1), channel_id=1, source_target_pairs={{0,128},{64,192},{128,256},{192,320},{256,384},{320,448},{384,512}... | collective-permute-start | bytes 1198088 | tf_op jit(solution)/shard_map/ppermute | solution.py:19
  53.9 0.8 copy-start.10
  70.3 2.9 copy-start.15
  74.8 1.3 copy-start.24
  77.3 18.9 %collective-permute-start.3 = (f32[24,65,64]{1,2,0:T(8,128)}, f32[24,65,64]{1,2,0:T(8,128)S(1)}, u32[]{:S(2)}, u32[]{:S(2)}) collective-permute-start(f32[24,65,64]{1,2,0:T(8,128)} %pad_maximum_fusion.2), channel_id=1, source_target_pairs={{0,256},{64,320},{128,384},{192,448},{256,512},{320,576},{384,640}... | collective-permute-start | bytes 1198088 | tf_op jit(solution)/shard_map/ppermute | solution.py:19
  86.6 240.6 %copy-start.19 = (s32[256]{0:T(256)}, s32[256]{0:T(256)S(1)}, u32[]{:S(2)}) copy-start(s32[256]{0:T(256)S(1)} %fusion.52) | copy-start | bytes 3076
  96.3 2.3 copy-start.14
  99.9 7.8 %copy-start.11 = (s32[1,128,2]{2,1,0:T(8,128)S(1)}, s32[1,128,2]{2,1,0:T(8,128)}, u32[]{:S(2)}) copy-start(s32[1,128,2]{2,1,0:T(8,128)} %copy-done.10) | copy-start | bytes 3076
  99.9 7.8 %copy-start.16 = (s32[1,128,2]{2,1,0:T(8,128)S(1)}, s32[1,128,2]{2,1,0:T(8,128)}, u32[]{:S(2)}) copy-start(s32[1,128,2]{2,1,0:T(8,128)} %reduce_sum.77) | copy-start | bytes 3076
  101.2 20.2 %collective-permute-start.4 = (f32[24,65,64]{1,2,0:T(8,128)}, f32[24,65,64]{1,2,0:T(8,128)}, u32[]{:S(2)}, u32[]{:S(2)}) collective-permute-start(f32[24,65,64]{1,2,0:T(8,128)} %pad_maximum_fusion.3), channel_id=1, source_target_pairs={{0,512},{64,576},{128,640},{192,704},{256,768},{320,832},{384,896}... | collective-permute-start | bytes 1198088 | tf_op jit(solution)/shard_map/ppermute | solution.py:19
  108.3 15.8 %copy-start.4 = (bf16[1,128,1536]{1,2,0:T(8,128)(2,1)S(1)}, bf16[1,128,1536]{1,2,0:T(8,128)(2,1)}, u32[]{:S(2)}) copy-start(bf16[1,128,1536]{1,2,0:T(8,128)(2,1)} %copy-done.3) | copy-start | bytes 1179652
  108.3 15.8 %copy-start.6 = (bf16[1,128,1536]{1,2,0:T(8,128)(2,1)S(1)}, bf16[1,128,1536]{1,2,0:T(8,128)(2,1)}, u32[]{:S(2)}) copy-start(bf16[1,128,1536]{1,2,0:T(8,128)(2,1)} %copy-done.5) | copy-start | bytes 1179652
  127.7 0.7 copy-start.17
  127.8 2.2 copy-start.1
  128.4 1.6 copy-start.9
  128.4 1.6 copy-start.22
  130.0 185.6 %copy-start.25 = (f32[128]{0:T(128)}, f32[128]{0:T(128)S(1)}, u32[]{:S(2)}) copy-start(f32[128]{0:T(128)S(1)} %add_rsqrt_fusion.1) | copy-start | bytes 1540
  130.7 184.9 %copy-start.26 = (bf16[1,1536,512]{2,1,0:T(8,128)(2,1)S(1)}, bf16[1,1536,512]{2,1,0:T(8,128)(2,1)}, u32[]{:S(2)}) copy-start(bf16[1,1536,512]{2,1,0:T(8,128)(2,1)} %param.23) | copy-start | bytes 4718596
  322.2 8.2 %copy-start.21 = (s32[1,128,2]{1,2,0:T(2,128)S(1)}, s32[1,128,2]{1,2,0:T(2,128)}, u32[]{:S(2)}) copy-start(s32[1,128,2]{1,2,0:T(2,128)} %param.22) | copy-start | bytes 3076
  322.2 160.6 %all-to-all-start.1 = ((bf16[64,8,1536]{2,1,0:T(8,128)(2,1)}), bf16[64,8,1536]{2,1,0:T(8,128)(2,1)S(1)}, u32[]{:S(2)}, u32[]{:S(2)}) async-start(bf16[64,8,1536]{2,1,0:T(8,128)(2,1)} %convolution_convert_fusion), calls=%async_computation.1 | async-start | bytes 3145728 | tf_op jit(solution)/shard_map/all_to_all | solution.py:143
  485.1 6.3 %copy-start.2 = (f32[1,128,1536]{2,1,0:T(8,128)S(1)}, f32[1,128,1536]{2,1,0:T(8,128)}, u32[]{:S(2)}) copy-start(f32[1,128,1536]{2,1,0:T(8,128)} %copy.51) | copy-start | bytes 2359300
  485.1 6.3 %copy-start.7 = (bf16[1,128,1536]{2,1,0:T(8,128)(2,1)S(1)}, bf16[1,128,1536]{2,1,0:T(8,128)(2,1)}, u32[]{:S(2)}) copy-start(bf16[1,128,1536]{2,1,0:T(8,128)(2,1)} %param.18) | copy-start | bytes 1179652
  487.4 4.0 copy-start.8
  487.4 4.0 copy-start.18

commit v3 on v2

--- a/solution.py
+++ b/solution.py
@@ -4,6 +4,53 @@
 from jax.sharding import PartitionSpec as P
 
 HIGHEST = lax.Precision.HIGHEST
+
+
+def entering_grid(block_decay, contribution, axis):
+    count, mine = (lax.axis_size(axis), lax.axis_index(axis))
+    width = int(round(count ** 0.5))
+    if width * width != count or width < 2:
+        return entering_scan(block_decay, contribution, axis)
+    rows = contribution.shape[1]
+    row_of, col_of = mine // width, mine % width
+
+    def pack(state, decay):
+        decay_row = jnp.broadcast_to(decay[:, None, None], state.shape[:1] + (1,) + state.shape[2:])
+        return jnp.concatenate([state, decay_row], axis=1)
+
+    def split(value):
+        return value[:, :rows], value[:, rows, 0]
+
+    def along_row(value, step):
+        pairs = [(i, (i // width) * width + (i % width + step) % width) for i in range(count)]
+        return split(lax.ppermute(value, axis, pairs))
+
+    def along_col(value, step):
+        pairs = [(i, ((i // width + step) % width) * width + i % width) for i in range(count)]
+        return split(lax.ppermute(value, axis, pairs))
+
+    def prefix(own_index, got):
+        state = jnp.zeros_like(got[0][0])
+        weight = jnp.ones_like(got[0][1])
+        for step, (got_state, got_decay) in enumerate(got, start=1):
+            has = own_index >= step
+            state = jnp.where(has, weight[:, None, None] * got_state + state, state)
+            weight = jnp.where(has, weight * got_decay, weight)
+        return state, weight
+
+    packed = pack(contribution, block_decay)
+    in_row = [along_row(packed, step) for step in range(1, width)]
+    before, before_decay = prefix(col_of, in_row)
+    total = block_decay[:, None, None] * before + contribution
+    total_decay = before_decay * block_decay
+    for ahead in range(1, width):
+        got_state, got_decay = in_row[width - 1 - ahead]
+        has = col_of + ahead <= width - 1
+        total = jnp.where(has, got_decay[:, None, None] * total + got_state, total)
+        total_decay = jnp.where(has, total_decay * got_decay, total_decay)
+    in_col = [along_col(pack(total, total_decay), step) for step in range(1, width)]
+    entering_row, _ = prefix(row_of, in_col)
+    return before_decay[:, None, None] * entering_row + before
 
 
 def entering_scan(block_decay, contribution, axis):
@@ -98,7 +145,7 @@
     contribution = jnp.einsum(
         "thd,the->hde", k_scaled, v_rows.astype(jnp.float32), precision=HIGHEST
     )
-    entering = entering_scan(block_decay, contribution, "ctx")
+    entering = entering_grid(block_decay, contribution, "ctx")
     carried = (
         jnp.einsum("thd,hde->the", q_rows.astype(jnp.float32), entering, precision=HIGHEST)
         * (inv_root * jnp.exp(cumulated)).T[:, :, None]

time: 501 us -> 473 us (0.944); the launches traced: 492 us -> 470 us
  waiting for transfers between devices: 207 us -> 182 us
  starting transfers between devices: 28.8 us -> 35 us
  other arithmetic: 34.2 us -> 28.2 us
    ppermute x5 -> x6, waiting for transfers between devices: 62.6 us -> 37.1 us  [the longest x3 26.2 us: along_col(): return split(lax.ppermute(value, axis, pairs))]
    ppermute x5 -> x6, starting transfers between devices: 23.8 us -> 30.2 us  [the longest x3 19.7 us: along_row(): return split(lax.ppermute(value, axis, pairs))]
    select_n x9 -> x3, other arithmetic: 11 us -> 5.55 us  [the longest x2 2.88 us: prefix(): weight = jnp.where(has, weight * got_decay, weight)]
  transfers between devices with their start and end apart: 6 -> 7, of which waited for: 6 -> 4; matrix products, arithmetic and copies ran while one was open for 5% -> 6% of each run, Pallas kernels for 0% -> 0%
where the time goes in v3:
time: 473 us; the launch traced here: 470 us
  blocking collectives  185 us (39%)
  waiting for transfers between devices  182 us (38%)
  starting transfers between devices  35 us (7%)
  other arithmetic  28.2 us (6%)
  local copies, waits for them, and re-layouts  23.3 us (5%)
  matrix products  16.5 us (3%)
    all_to_all x1, blocking collectives, on_device(): lax.all_to_all(outgoing, 'exp', split_axis=0, concat_axis=0, tiled=True)  185 us
    all_to_all x1, waiting for transfers between devices, on_device(): lax.all_to_all(produced, 'exp', split_axis=0, concat_axis=0, tiled=True)  145 us
    ppermute x3, waiting for transfers between devices, along_col(): return split(lax.ppermute(value, axis, pairs))  26.2 us
    ppermute x3, starting transfers between devices, along_row(): return split(lax.ppermute(value, axis, pairs))  19.7 us
    ppermute x3, waiting for transfers between devices, along_row(): return split(lax.ppermute(value, axis, pairs))  10.9 us
    ppermute x3, starting transfers between devices, along_col(): return split(lax.ppermute(value, axis, pairs))  10.5 us
  transfers between devices with their start and end apart: 7, of which 4 were waited for; matrix products, arithmetic and copies ran while one was open for 6% of the time, Pallas kernels for 0%

profile of v3, /device:TPU:6, one launch (start us, length us, event | category | flops | bytes accessed | tf_op | source)
XLA Modules:
  0.0 470.2 jit_solution(10199748627987746852)
XLA Ops:
  0.0 1.1 reduce_window_sum.26
  1.1 0.8 slice_reduce_fusion.1
  2.5 1.2 copy.52
  3.7 1.2 copy.53
  5.0 0.8 fusion.38
  5.9 1.2 pad_maximum_fusion
  7.1 15.0 %collective-permute-start = (f32[24,65,64]{1,2,0:T(8,128)}, f32[24,65,64]{1,2,0:T(8,128)S(1)}, u32[]{:S(2)}, u32[]{:S(2)}) collective-permute-start(f32[24,65,64]{1,2,0:T(8,128)} %pad_maximum_fusion), channel_id=1, source_target_pairs={{0,64},{64,128},{128,192},{192,0},{256,320},{320,384},{384,448},{4... | collective-permute-start | bytes 1198088 | tf_op jit(solution)/shard_map/ppermute | solution.py:26
  22.1 1.9 collective-permute-start.1
  24.0 2.8 collective-permute-start.2
  27.5 1.0 eq.62
  29.1 2.0 reduce-window.6
  31.1 1.6 slice_reduce_fusion
  32.7 1.2 exp.48
  33.9 1.5 reshape_reshape.3
  36.1 0.9 fusion.68
  37.0 0.8 reduce_sum.77
  37.8 10.9 %collective-permute-done = f32[24,65,64]{1,2,0:T(8,128)S(1)} collective-permute-done((f32[24,65,64]{1,2,0:T(8,128)}, f32[24,65,64]{1,2,0:T(8,128)S(1)}, u32[]{:S(2)}, u32[]{:S(2)}) %collective-permute-start) | collective-permute-done | bytes 399392 | tf_op jit(solution)/shard_map/ppermute | solution.py:26
  48.7 1.3 fusion.80
  50.0 2.0 slice_reduce_fusion.4
  52.1 2.7 add_select_fusion.4
  54.9 1.2 pad_maximum_fusion.1
  56.1 2.4 collective-permute-start.3
  58.5 4.8 %collective-permute-start.4 = (f32[24,65,64]{1,2,0:T(8,128)}, f32[24,65,64]{1,2,0:T(8,128)}, u32[]{:S(2)}, u32[]{:S(2)}) collective-permute-start(f32[24,65,64]{1,2,0:T(8,128)} %pad_maximum_fusion.1), channel_id=1, source_target_pairs={{0,512},{64,576},{128,640},{192,704},{256,768},{320,832},{384,896}... | collective-permute-start | bytes 1198088 | tf_op jit(solution)/shard_map/ppermute | solution.py:30
  63.4 3.3 collective-permute-start.5
  67.5 0.9 copy.64
  69.1 0.8 convert_reduce_fusion
  69.8 8.2 %collective-permute-done.3 = f32[24,65,64]{1,2,0:T(8,128)} collective-permute-done((f32[24,65,64]{1,2,0:T(8,128)}, f32[24,65,64]{1,2,0:T(8,128)}, u32[]{:S(2)}, u32[]{:S(2)}) %collective-permute-start.3) | collective-permute-done | bytes 399392 | tf_op jit(solution)/shard_map/ppermute | solution.py:30
  78.0 18.0 %collective-permute-done.4 = f32[24,65,64]{1,2,0:T(8,128)} collective-permute-done((f32[24,65,64]{1,2,0:T(8,128)}, f32[24,65,64]{1,2,0:T(8,128)}, u32[]{:S(2)}, u32[]{:S(2)}) %collective-permute-start.4) | collective-permute-done | bytes 399392 | tf_op jit(solution)/shard_map/ppermute | solution.py:30
  96.0 1.6 fusion.70
  97.6 4.0 fusion.16
  101.6 3.2 multiply_reduce_fusion.1
  104.8 1.2 broadcast_multiply_fusion
  106.3 1.5 fusion.31
  108.6 184.9 %all_to_all.10 = bf16[64,8,1536]{2,1,0:T(8,128)(2,1)S(1)} all-to-all(bf16[64,8,1536]{2,1,0:T(8,128)(2,1)S(1)} %fusion), channel_id=1, replica_groups=mesh['ctx'=16,'exp'=64] {'exp'}, dimensions={0} | all-to-all | bytes 3145728 | tf_op jit(solution)/shard_map/all_to_all | solution.py:188
  293.5 2.0 fusion.6
  295.5 4.7 convolution_convert_fusion
  300.1 4.8 %all-to-all-start.1 = ((bf16[64,8,1536]{2,1,0:T(8,128)(2,1)}), bf16[64,8,1536]{2,1,0:T(8,128)(2,1)S(1)}, u32[]{:S(2)}, u32[]{:S(2)}) async-start(bf16[64,8,1536]{2,1,0:T(8,128)(2,1)} %convolution_convert_fusion), calls=%async_computation.1 | async-start | bytes 3145728 | tf_op jit(solution)/shard_map/all_to_all | solution.py:190
  305.0 0.8 reduce_sum.76
  305.7 1.6 mul.326
  307.3 0.9 copy.61
  308.8 0.8 copy.62
  310.8 1.3 fusion.25
  313.6 2.3 copy.55
  315.9 144.7 %all-to-all-done.1 = bf16[64,8,1536]{2,1,0:T(8,128)(2,1)S(1)} async-done(((bf16[64,8,1536]{2,1,0:T(8,128)(2,1)}), bf16[64,8,1536]{2,1,0:T(8,128)(2,1)S(1)}, u32[]{:S(2)}, u32[]{:S(2)}) %all-to-all-start.1) | async-done | bytes 1572896 | tf_op jit(solution)/shard_map/all_to_all | solution.py:190
  460.6 2.3 gather_fusion
  462.9 2.3 gather.7
  465.2 4.0 multiply_reduce_fusion
  469.2 1.0 fusion.37
  (67 shorter events, 8.7 us)
Async XLA Ops:
  0.0 295.5 %copy-start = (bf16[1,512,1536]{2,1,0:T(8,128)(2,1)S(1)}, bf16[1,512,1536]{2,1,0:T(8,128)(2,1)}, u32[]{:S(2)}) copy-start(bf16[1,512,1536]{2,1,0:T(8,128)(2,1)} %param.25) | copy-start | bytes 4718596
  1.9 3.8 copy-start.19
  5.0 0.9 copy-start.3
  5.7 21.0 %copy-start.14 = (s32[1,128,2]{1,2,0:T(2,128)S(1)}, s32[1,128,2]{1,2,0:T(2,128)}, u32[]{:S(2)}) copy-start(s32[1,128,2]{1,2,0:T(2,128)} %param.22) | copy-start | bytes 3076
  7.1 41.7 %collective-permute-start = (f32[24,65,64]{1,2,0:T(8,128)}, f32[24,65,64]{1,2,0:T(8,128)S(1)}, u32[]{:S(2)}, u32[]{:S(2)}) collective-permute-start(f32[24,65,64]{1,2,0:T(8,128)} %pad_maximum_fusion), channel_id=1, source_target_pairs={{0,64},{64,128},{128,192},{192,0},{256,320},{320,384},{384,448},{4... | collective-permute-start | bytes 1198088 | tf_op jit(solution)/shard_map/ppermute | solution.py:26
  22.1 26.7 %collective-permute-start.1 = (f32[24,65,64]{1,2,0:T(8,128)}, f32[24,65,64]{1,2,0:T(8,128)}, u32[]{:S(2)}, u32[]{:S(2)}) collective-permute-start(f32[24,65,64]{1,2,0:T(8,128)} %pad_maximum_fusion), channel_id=1, source_target_pairs={{0,128},{64,192},{128,0},{192,64},{256,384},{320,448},{384,256},{4... | collective-permute-start | bytes 1198088 | tf_op jit(solution)/shard_map/ppermute | solution.py:26
  24.0 26.0 %collective-permute-start.2 = (f32[24,65,64]{1,2,0:T(8,128)}, f32[24,65,64]{1,2,0:T(8,128)}, u32[]{:S(2)}, u32[]{:S(2)}) collective-permute-start(f32[24,65,64]{1,2,0:T(8,128)} %pad_maximum_fusion), channel_id=1, source_target_pairs={{0,192},{64,0},{128,64},{192,128},{256,448},{320,256},{384,320},{4... | collective-permute-start | bytes 1198088 | tf_op jit(solution)/shard_map/ppermute | solution.py:26
  37.0 268.0 %copy-start.13 = (s32[256]{0:T(256)}, s32[256]{0:T(256)S(1)}, u32[]{:S(2)}) copy-start(s32[256]{0:T(256)S(1)} %fusion.68) | copy-start | bytes 3076
  50.0 4.7 %copy-start.17 = (f32[24]{0:T(128)}, f32[24]{0:T(128)S(1)}, u32[]{:S(2)}) copy-start(f32[24]{0:T(128)S(1)} %get-tuple-element.19) | copy-start | bytes 292
  52.1 2.7 copy-start.18
  54.8 11.9 %copy-start.8 = (s32[1,128,2]{2,1,0:T(8,128)S(1)}, s32[1,128,2]{2,1,0:T(8,128)}, u32[]{:S(2)}) copy-start(s32[1,128,2]{2,1,0:T(8,128)} %copy.58) | copy-start | bytes 3076
  54.8 11.9 %copy-start.10 = (s32[1,128,2]{2,1,0:T(8,128)S(1)}, s32[1,128,2]{2,1,0:T(8,128)}, u32[]{:S(2)}) copy-start(s32[1,128,2]{2,1,0:T(8,128)} %reduce_sum.77) | copy-start | bytes 3076
  54.8 12.5 %copy-start.9 = (bf16[1,128,1536]{2,1,0:T(8,128)(2,1)S(1)}, bf16[1,128,1536]{2,1,0:T(8,128)(2,1)}, u32[]{:S(2)}) copy-start(bf16[1,128,1536]{2,1,0:T(8,128)(2,1)} %param.13) | copy-start | bytes 1179652
  56.1 21.9 %collective-permute-start.3 = (f32[24,65,64]{1,2,0:T(8,128)}, f32[24,65,64]{1,2,0:T(8,128)}, u32[]{:S(2)}, u32[]{:S(2)}) collective-permute-start(f32[24,65,64]{1,2,0:T(8,128)} %pad_maximum_fusion.1), channel_id=1, source_target_pairs={{0,256},{64,320},{128,384},{192,448},{256,512},{320,576},{384,640}... | collective-permute-start | bytes 1198088 | tf_op jit(solution)/shard_map/ppermute | solution.py:30
  58.5 37.5 %collective-permute-start.4 = (f32[24,65,64]{1,2,0:T(8,128)}, f32[24,65,64]{1,2,0:T(8,128)}, u32[]{:S(2)}, u32[]{:S(2)}) collective-permute-start(f32[24,65,64]{1,2,0:T(8,128)} %pad_maximum_fusion.1), channel_id=1, source_target_pairs={{0,512},{64,576},{128,640},{192,704},{256,768},{320,832},{384,896}... | collective-permute-start | bytes 1198088 | tf_op jit(solution)/shard_map/ppermute | solution.py:30
  63.4 34.2 %collective-permute-start.5 = (f32[24,65,64]{1,2,0:T(8,128)}, f32[24,65,64]{1,2,0:T(8,128)}, u32[]{:S(2)}, u32[]{:S(2)}) collective-permute-start(f32[24,65,64]{1,2,0:T(8,128)} %pad_maximum_fusion.1), channel_id=1, source_target_pairs={{0,768},{64,832},{128,896},{192,960},{256,0},{320,64},{384,128},{4... | collective-permute-start | bytes 1198088 | tf_op jit(solution)/shard_map/ppermute | solution.py:30
  97.6 4.0 copy-start.4
  104.8 1.5 copy-start.11
  106.0 1.9 copy-start.1
  106.3 1.6 copy-start.7
  106.3 1.6 copy-start.16
  107.9 185.6 %copy-start.20 = (f32[128]{0:T(128)}, f32[128]{0:T(128)S(1)}, u32[]{:S(2)}) copy-start(f32[128]{0:T(128)S(1)} %add_rsqrt_fusion.1) | copy-start | bytes 1540
  108.6 184.9 %copy-start.21 = (bf16[1,1536,512]{2,1,0:T(8,128)(2,1)S(1)}, bf16[1,1536,512]{2,1,0:T(8,128)(2,1)}, u32[]{:S(2)}) copy-start(bf16[1,1536,512]{2,1,0:T(8,128)(2,1)} %param.23) | copy-start | bytes 4718596
  300.1 8.1 %copy-start.15 = (s32[1,128,2]{1,2,0:T(2,128)S(1)}, s32[1,128,2]{1,2,0:T(2,128)}, u32[]{:S(2)}) copy-start(s32[1,128,2]{1,2,0:T(2,128)} %param.22) | copy-start | bytes 3076
  300.1 160.4 %all-to-all-start.1 = ((bf16[64,8,1536]{2,1,0:T(8,128)(2,1)}), bf16[64,8,1536]{2,1,0:T(8,128)(2,1)S(1)}, u32[]{:S(2)}, u32[]{:S(2)}) async-start(bf16[64,8,1536]{2,1,0:T(8,128)(2,1)} %convolution_convert_fusion), calls=%async_computation.1 | async-start | bytes 3145728 | tf_op jit(solution)/shard_map/all_to_all | solution.py:190
  462.9 6.3 %copy-start.2 = (f32[1,128,1536]{2,1,0:T(8,128)S(1)}, f32[1,128,1536]{2,1,0:T(8,128)}, u32[]{:S(2)}) copy-start(f32[1,128,1536]{2,1,0:T(8,128)} %copy.55) | copy-start | bytes 2359300
  462.9 6.3 %copy-start.5 = (bf16[1,128,1536]{2,1,0:T(8,128)(2,1)S(1)}, bf16[1,128,1536]{2,1,0:T(8,128)(2,1)}, u32[]{:S(2)}) copy-start(bf16[1,128,1536]{2,1,0:T(8,128)(2,1)} %param.18) | copy-start | bytes 1179652
  465.1 4.0 copy-start.6
  465.1 4.0 copy-start.12

commit v4 on v3

--- a/solution.py
+++ b/solution.py
@@ -15,11 +15,15 @@
     row_of, col_of = mine // width, mine % width
 
     def pack(state, decay):
-        decay_row = jnp.broadcast_to(decay[:, None, None], state.shape[:1] + (1,) + state.shape[2:])
-        return jnp.concatenate([state, decay_row], axis=1)
+        high = decay.astype(jnp.bfloat16)
+        low = (decay - high.astype(jnp.float32)).astype(jnp.bfloat16)
+        shape = state.shape[:1] + (1,) + state.shape[2:]
+        decay_rows = [jnp.broadcast_to(part[:, None, None], shape) for part in (high, low)]
+        return jnp.concatenate([state.astype(jnp.bfloat16)] + decay_rows, axis=1)
 
     def split(value):
-        return value[:, :rows], value[:, rows, 0]
+        decay = value[:, rows, 0].astype(jnp.float32) + value[:, rows + 1, 0].astype(jnp.float32)
+        return value[:, :rows].astype(jnp.float32), decay
 
     def along_row(value, step):
         pairs = [(i, (i // width) * width + (i % width + step) % width) for i in range(count)]

time: 473 us -> 438 us (0.926)
  waiting for transfers between devices: 182 us -> 157 us
  local copies, waits for them, and re-layouts: 23.3 us -> 18.2 us
    ppermute x3, waiting for transfers between devices: 26.2 us -> 9.16 us  [along_col(): return split(lax.ppermute(value, axis, pairs))]
    ppermute x3, waiting for transfers between devices: 10.9 us -> 2.75 us  [along_row(): return split(lax.ppermute(value, axis, pairs))]
  transfers between devices with their start and end apart: 7 -> 7, of which waited for: 4 -> 5; matrix products, arithmetic and copies ran while one was open for 6% -> 4% of each run, Pallas kernels for 0% -> 0%
where the time goes in v4:
time: 438 us; the launch traced here: 433 us
  blocking collectives  185 us (42%)
  waiting for transfers between devices  157 us (36%)
  starting transfers between devices  34.1 us (8%)
  other arithmetic  23.7 us (5%)
  local copies, waits for them, and re-layouts  18.2 us (4%)
  matrix products  15.7 us (4%)
    all_to_all x1, blocking collectives, on_device(): lax.all_to_all(outgoing, 'exp', split_axis=0, concat_axis=0, tiled=True)  185 us
    all_to_all x1, waiting for transfers between devices, on_device(): lax.all_to_all(produced, 'exp', split_axis=0, concat_axis=0, tiled=True)  145 us
    ppermute x3, starting transfers between devices, along_row(): return split(lax.ppermute(value, axis, pairs))  20.3 us
    ppermute x3, waiting for transfers between devices, along_col(): return split(lax.ppermute(value, axis, pairs))  9.16 us
    ppermute x3, starting transfers between devices, along_col(): return split(lax.ppermute(value, axis, pairs))  9 us
  transfers between devices with their start and end apart: 7, of which 5 were waited for; matrix products, arithmetic and copies ran while one was open for 4% of the time, Pallas kernels for 0%

profile of v4, /device:TPU:6, one launch (start us, length us, event | category | flops | bytes accessed | tf_op | source)
XLA Modules:
  0.0 433.3 jit_solution(6481449483708184696)
XLA Ops:
  0.0 1.1 reduce_window_sum.26
  1.1 0.8 slice_exponential_fusion
  3.1 1.2 copy.52
  4.3 1.2 copy.53
  5.5 0.8 fusion.102
  6.6 1.1 pad_maximum_fusion
  7.7 2.7 collective-permute-start.2
  10.4 15.6 %collective-permute-start.1 = (bf16[24,66,64]{1,2,0:T(8,128)(2,1)}, bf16[24,66,64]{1,2,0:T(8,128)(2,1)}, u32[]{:S(2)}, u32[]{:S(2)}) collective-permute-start(bf16[24,66,64]{1,2,0:T(8,128)(2,1)} %pad_maximum_fusion), channel_id=1, source_target_pairs={{0,128},{64,192},{128,0},{192,64},{256,384},{320,448},{384,256},{4... | collective-permute-start | bytes 608264 | tf_op jit(solution)/shard_map/ppermute | solution.py:30
  26.1 1.9 collective-permute-start
  28.5 0.6 reduce-window.6
  29.6 0.6 broadcast_multiply_fusion.1
  30.2 0.6 copy.64
  30.8 1.2 copy.51
  32.1 2.4 collective-permute-done.1
  34.4 1.2 fusion.97
  36.1 1.5 fusion.94
  37.6 1.0 fusion.95
  38.8 2.7 fusion.34
  42.2 2.0 collective-permute-start.4
  44.2 2.6 collective-permute-start.3
  46.8 0.8 convert_reduce_fusion
  47.5 4.5 %collective-permute-start.5 = (bf16[24,66,64]{1,2,0:T(8,128)(2,1)S(1)}, bf16[24,66,64]{1,2,0:T(8,128)(2,1)S(1)}, u32[]{:S(2)}, u32[]{:S(2)}) collective-permute-start(bf16[24,66,64]{1,2,0:T(8,128)(2,1)S(1)} %pad_maximum_fusion.1), channel_id=1, source_target_pairs={{0,768},{64,832},{128,896},{192,960},{256,0},{320,64},{384,128},{4... | collective-permute-start | bytes 608264 | tf_op jit(solution)/shard_map/ppermute | solution.py:34
  52.0 4.7 %collective-permute-done.4 = bf16[24,66,64]{1,2,0:T(8,128)(2,1)S(1)} collective-permute-done((bf16[24,66,64]{1,2,0:T(8,128)(2,1)S(1)}, bf16[24,66,64]{1,2,0:T(8,128)(2,1)S(1)}, u32[]{:S(2)}, u32[]{:S(2)}) %collective-permute-start.4) | collective-permute-done | bytes 202784 | tf_op jit(solution)/shard_map/ppermute | solution.py:34
  56.7 4.5 %collective-permute-done.3 = bf16[24,66,64]{1,2,0:T(8,128)(2,1)S(1)} collective-permute-done((bf16[24,66,64]{1,2,0:T(8,128)(2,1)S(1)}, bf16[24,66,64]{1,2,0:T(8,128)(2,1)S(1)}, u32[]{:S(2)}, u32[]{:S(2)}) %collective-permute-start.3) | collective-permute-done | bytes 202784 | tf_op jit(solution)/shard_map/ppermute | solution.py:34
  61.2 0.6 fusion.88
  61.8 3.2 fusion.16
  65.1 3.2 multiply_reduce_fusion.1
  68.3 1.2 broadcast_multiply_fusion
  69.8 1.5 fusion.35
  71.4 0.6 fusion
  72.0 184.6 %all_to_all.10 = bf16[64,8,1536]{2,1,0:T(8,128)(2,1)S(1)} all-to-all(bf16[64,8,1536]{2,1,0:T(8,128)(2,1)S(1)} %fusion), channel_id=1, replica_groups=mesh['ctx'=16,'exp'=64] {'exp'}, dimensions={0} | all-to-all | bytes 3145728 | tf_op jit(solution)/shard_map/all_to_all | solution.py:192
  256.6 2.0 fusion.6
  258.6 4.7 %convolution_convert_fusion = bf16[64,8,1536]{2,1,0:T(8,128)(2,1)} fusion(bf16[1,512,1536]{2,1,0:T(8,128)(2,1)S(1)} %copy-done, bf16[64,8,1536]{2,1,0:T(8,128)(2,1)S(1)} %all_to_all.10, bf16[1,1536,512]{2,1,0:T(8,128)(2,1)} %param.24, f32[64,1,8,512]{3,2,0,1:T(8,128)} %fusion.6), kind=kOutput, calls=%fused_computation.1 | convolution fusion | flops 1612972032 | bytes 7340032 | tf_op jit(solution)/shard_map/senf,efd->send/dot_general | solution.py:104
  263.3 4.8 %all-to-all-start.1 = ((bf16[64,8,1536]{2,1,0:T(8,128)(2,1)}), bf16[64,8,1536]{2,1,0:T(8,128)(2,1)S(1)}, u32[]{:S(2)}, u32[]{:S(2)}) async-start(bf16[64,8,1536]{2,1,0:T(8,128)(2,1)} %convolution_convert_fusion), calls=%async_computation.1 | async-start | bytes 3145728 | tf_op jit(solution)/shard_map/all_to_all | solution.py:194
  268.1 0.8 reduce_sum.76
  268.8 1.6 mul.332
  270.4 0.9 copy.61
  271.8 0.8 copy.62
  272.6 0.7 compare_select_fusion
  273.9 2.3 copy.55
  276.2 1.3 fusion.25
  277.5 0.7 select_reduce_fusion
  278.2 0.7 copy.57
  279.0 144.7 %all-to-all-done.1 = bf16[64,8,1536]{2,1,0:T(8,128)(2,1)S(1)} async-done(((bf16[64,8,1536]{2,1,0:T(8,128)(2,1)}), bf16[64,8,1536]{2,1,0:T(8,128)(2,1)S(1)}, u32[]{:S(2)}, u32[]{:S(2)}) %all-to-all-start.1) | async-done | bytes 1572896 | tf_op jit(solution)/shard_map/all_to_all | solution.py:194
  423.7 2.3 gather_fusion
  426.0 2.3 gather.7
  428.3 4.0 multiply_reduce_fusion
  432.3 1.0 fusion.41
  (59 shorter events, 5.1 us)
Async XLA Ops:
  0.0 258.6 %copy-start = (bf16[1,512,1536]{2,1,0:T(8,128)(2,1)S(1)}, bf16[1,512,1536]{2,1,0:T(8,128)(2,1)}, u32[]{:S(2)}) copy-start(bf16[1,512,1536]{2,1,0:T(8,128)(2,1)} %param.25) | copy-start | bytes 4718596
  6.3 21.7 %copy-start.10 = (s32[1,128,2]{1,2,0:T(2,128)S(1)}, s32[1,128,2]{1,2,0:T(2,128)}, u32[]{:S(2)}) copy-start(s32[1,128,2]{1,2,0:T(2,128)} %param.22) | copy-start | bytes 3076
  7.7 28.0 %collective-permute-start.2 = (bf16[24,66,64]{1,2,0:T(8,128)(2,1)}, bf16[24,66,64]{1,2,0:T(8,128)(2,1)}, u32[]{:S(2)}, u32[]{:S(2)}) collective-permute-start(bf16[24,66,64]{1,2,0:T(8,128)(2,1)} %pad_maximum_fusion), channel_id=1, source_target_pairs={{0,192},{64,0},{128,64},{192,128},{256,448},{320,256},{384,320},{4... | collective-permute-start | bytes 608264 | tf_op jit(solution)/shard_map/ppermute | solution.py:30
  10.4 24.0 %collective-permute-start.1 = (bf16[24,66,64]{1,2,0:T(8,128)(2,1)}, bf16[24,66,64]{1,2,0:T(8,128)(2,1)}, u32[]{:S(2)}, u32[]{:S(2)}) collective-permute-start(bf16[24,66,64]{1,2,0:T(8,128)(2,1)} %pad_maximum_fusion), channel_id=1, source_target_pairs={{0,128},{64,192},{128,0},{192,64},{256,384},{320,448},{384,256},{4... | collective-permute-start | bytes 608264 | tf_op jit(solution)/shard_map/ppermute | solution.py:30
  26.1 10.0 %collective-permute-start = (bf16[24,66,64]{1,2,0:T(8,128)(2,1)}, bf16[24,66,64]{1,2,0:T(8,128)(2,1)}, u32[]{:S(2)}, u32[]{:S(2)}) collective-permute-start(bf16[24,66,64]{1,2,0:T(8,128)(2,1)} %pad_maximum_fusion), channel_id=1, source_target_pairs={{0,64},{64,128},{128,192},{192,0},{256,320},{320,384},{384,448},{4... | collective-permute-start | bytes 608264 | tf_op jit(solution)/shard_map/ppermute | solution.py:30
  29.4 238.6 %copy-start.8 = (s32[256]{0:T(256)}, s32[256]{0:T(256)S(1)}, u32[]{:S(2)}) copy-start(s32[256]{0:T(256)S(1)} %fusion.81) | copy-start | bytes 3076
  41.6 5.2 %copy-start.13 = (s32[128,2]{0,1:T(2,128)S(1)}, s32[128,2]{0,1:T(2,128)}, u32[]{:S(2)}) copy-start(s32[128,2]{0,1:T(2,128)} %copy.64) | copy-start | bytes 3076
  41.6 20.3 %copy-start.9 = (f32[128,24]{0,1:T(8,128)S(1)}, f32[128,24]{0,1:T(8,128)}, u32[]{:S(2)}) copy-start(f32[128,24]{0,1:T(8,128)} %get-tuple-element.25) | copy-start | bytes 36868
  42.2 14.5 %collective-permute-start.4 = (bf16[24,66,64]{1,2,0:T(8,128)(2,1)S(1)}, bf16[24,66,64]{1,2,0:T(8,128)(2,1)S(1)}, u32[]{:S(2)}, u32[]{:S(2)}) collective-permute-start(bf16[24,66,64]{1,2,0:T(8,128)(2,1)S(1)} %pad_maximum_fusion.1), channel_id=1, source_target_pairs={{0,512},{64,576},{128,640},{192,704},{256,768},{320,832},{384,896}... | collective-permute-start | bytes 608264 | tf_op jit(solution)/shard_map/ppermute | solution.py:34
  44.2 17.0 %collective-permute-start.3 = (bf16[24,66,64]{1,2,0:T(8,128)(2,1)S(1)}, bf16[24,66,64]{1,2,0:T(8,128)(2,1)S(1)}, u32[]{:S(2)}, u32[]{:S(2)}) collective-permute-start(bf16[24,66,64]{1,2,0:T(8,128)(2,1)S(1)} %pad_maximum_fusion.1), channel_id=1, source_target_pairs={{0,256},{64,320},{128,384},{192,448},{256,512},{320,576},{384,640}... | collective-permute-start | bytes 608264 | tf_op jit(solution)/shard_map/ppermute | solution.py:34
  47.5 14.3 %collective-permute-start.5 = (bf16[24,66,64]{1,2,0:T(8,128)(2,1)S(1)}, bf16[24,66,64]{1,2,0:T(8,128)(2,1)S(1)}, u32[]{:S(2)}, u32[]{:S(2)}) collective-permute-start(bf16[24,66,64]{1,2,0:T(8,128)(2,1)S(1)} %pad_maximum_fusion.1), channel_id=1, source_target_pairs={{0,768},{64,832},{128,896},{192,960},{256,0},{320,64},{384,128},{4... | collective-permute-start | bytes 608264 | tf_op jit(solution)/shard_map/ppermute | solution.py:34
  68.2 1.5 copy-start.6
  69.5 1.9 copy-start.1
  69.8 1.6 copy-start.5
  69.8 1.6 copy-start.12
  71.4 185.3 %copy-start.14 = (f32[128]{0:T(128)}, f32[128]{0:T(128)S(1)}, u32[]{:S(2)}) copy-start(f32[128]{0:T(128)S(1)} %add_rsqrt_fusion.1) | copy-start | bytes 1540
  72.0 184.6 %copy-start.15 = (bf16[1,1536,512]{2,1,0:T(8,128)(2,1)S(1)}, bf16[1,1536,512]{2,1,0:T(8,128)(2,1)}, u32[]{:S(2)}) copy-start(bf16[1,1536,512]{2,1,0:T(8,128)(2,1)} %param.23) | copy-start | bytes 4718596
  263.3 8.0 %copy-start.11 = (s32[1,128,2]{1,2,0:T(2,128)S(1)}, s32[1,128,2]{1,2,0:T(2,128)}, u32[]{:S(2)}) copy-start(s32[1,128,2]{1,2,0:T(2,128)} %param.22) | copy-start | bytes 3076
  263.3 160.4 %all-to-all-start.1 = ((bf16[64,8,1536]{2,1,0:T(8,128)(2,1)}), bf16[64,8,1536]{2,1,0:T(8,128)(2,1)S(1)}, u32[]{:S(2)}, u32[]{:S(2)}) async-start(bf16[64,8,1536]{2,1,0:T(8,128)(2,1)} %convolution_convert_fusion), calls=%async_computation.1 | async-start | bytes 3145728 | tf_op jit(solution)/shard_map/all_to_all | solution.py:194
  426.0 6.3 %copy-start.2 = (f32[1,128,1536]{2,1,0:T(8,128)S(1)}, f32[1,128,1536]{2,1,0:T(8,128)}, u32[]{:S(2)}) copy-start(f32[1,128,1536]{2,1,0:T(8,128)} %copy.55) | copy-start | bytes 2359300
  426.0 6.3 %copy-start.3 = (bf16[1,128,1536]{2,1,0:T(8,128)(2,1)S(1)}, bf16[1,128,1536]{2,1,0:T(8,128)(2,1)}, u32[]{:S(2)}) copy-start(bf16[1,128,1536]{2,1,0:T(8,128)(2,1)} %param.18) | copy-start | bytes 1179652
  428.2 4.0 copy-start.4
  428.3 4.0 copy-start.7

commit v5 on v4

--- a/solution.py
+++ b/solution.py
@@ -30,7 +30,7 @@
         return split(lax.ppermute(value, axis, pairs))
 
     def along_col(value, step):
-        pairs = [(i, ((i // width + step) % width) * width + i % width) for i in range(count)]
+        pairs = [(i, (i // width + step) * width + i % width) for i in range(count - step * width)]
         return split(lax.ppermute(value, axis, pairs))
 
     def prefix(own_index, got):

time: 438 us -> 438 us (level)
  no operation moved by 1% of the time
where the time goes in v5:
time: 438 us; the launch traced here: 433 us
  blocking collectives  185 us (42%)
  waiting for transfers between devices  159 us (36%)
  starting transfers between devices  31 us (7%)
  other arithmetic  23.7 us (5%)
  local copies, waits for them, and re-layouts  18.2 us (4%)
  matrix products  15.7 us (4%)
    all_to_all x1, blocking collectives, on_device(): lax.all_to_all(outgoing, 'exp', split_axis=0, concat_axis=0, tiled=True)  185 us
    all_to_all x1, waiting for transfers between devices, on_device(): lax.all_to_all(produced, 'exp', split_axis=0, concat_axis=0, tiled=True)  145 us
    ppermute x3, starting transfers between devices, along_row(): return split(lax.ppermute(value, axis, pairs))  20.3 us
    ppermute x3, waiting for transfers between devices, along_col(): return split(lax.ppermute(value, axis, pairs))  11.2 us
  transfers between devices with their start and end apart: 7, of which 5 were waited for; matrix products, arithmetic and copies ran while one was open for 4% of the time, Pallas kernels for 0%

profile of v5, /device:TPU:6, one launch (start us, length us, event | category | flops | bytes accessed | tf_op | source)
XLA Modules:
  0.0 432.6 jit_solution(10812976535795367274)
XLA Ops:
  0.0 1.1 reduce_window_sum.26
  1.1 0.8 slice_exponential_fusion
  3.1 1.2 copy.52
  4.3 1.2 copy.53
  5.5 0.8 fusion.102
  6.6 1.1 pad_maximum_fusion
  7.7 2.7 collective-permute-start.2
  10.4 15.6 %collective-permute-start.1 = (bf16[24,66,64]{1,2,0:T(8,128)(2,1)}, bf16[24,66,64]{1,2,0:T(8,128)(2,1)}, u32[]{:S(2)}, u32[]{:S(2)}) collective-permute-start(bf16[24,66,64]{1,2,0:T(8,128)(2,1)} %pad_maximum_fusion), channel_id=1, source_target_pairs={{0,128},{64,192},{128,0},{192,64},{256,384},{320,448},{384,256},{4... | collective-permute-start | bytes 608264 | tf_op jit(solution)/shard_map/ppermute | solution.py:30
  26.1 1.9 collective-permute-start
  28.5 0.6 reduce-window.6
  29.6 0.6 broadcast_multiply_fusion.1
  30.2 0.6 copy.64
  30.8 1.2 copy.51
  32.1 2.4 collective-permute-done.1
  34.4 1.2 fusion.97
  36.1 1.5 fusion.94
  37.6 1.0 fusion.95
  38.8 2.7 fusion.34
  42.2 2.0 collective-permute-start.4
  44.2 2.6 collective-permute-start.3
  46.8 0.8 convert_reduce_fusion
  47.6 1.3 collective-permute-start.5
  48.9 4.8 %collective-permute-done.4 = bf16[24,66,64]{1,2,0:T(8,128)(2,1)S(1)} collective-permute-done((bf16[24,66,64]{1,2,0:T(8,128)(2,1)S(1)}, bf16[24,66,64]{1,2,0:T(8,128)(2,1)S(1)}, u32[]{:S(2)}, u32[]{:S(2)}) %collective-permute-start.4) | collective-permute-done | bytes 202784 | tf_op jit(solution)/shard_map/ppermute | solution.py:34
  53.7 6.4 %collective-permute-done.3 = bf16[24,66,64]{1,2,0:T(8,128)(2,1)S(1)} collective-permute-done((bf16[24,66,64]{1,2,0:T(8,128)(2,1)S(1)}, bf16[24,66,64]{1,2,0:T(8,128)(2,1)S(1)}, u32[]{:S(2)}, u32[]{:S(2)}) %collective-permute-start.3) | collective-permute-done | bytes 202784 | tf_op jit(solution)/shard_map/ppermute | solution.py:34
  60.1 0.6 fusion.88
  60.8 3.2 fusion.16
  64.0 3.2 multiply_reduce_fusion.1
  67.2 1.2 broadcast_multiply_fusion
  68.7 1.5 fusion.35
  70.3 0.6 fusion
  71.0 184.9 %all_to_all.10 = bf16[64,8,1536]{2,1,0:T(8,128)(2,1)S(1)} all-to-all(bf16[64,8,1536]{2,1,0:T(8,128)(2,1)S(1)} %fusion), channel_id=1, replica_groups=mesh['ctx'=16,'exp'=64] {'exp'}, dimensions={0} | all-to-all | bytes 3145728 | tf_op jit(solution)/shard_map/all_to_all | solution.py:192
  255.9 2.0 fusion.6
  257.8 4.7 %convolution_convert_fusion = bf16[64,8,1536]{2,1,0:T(8,128)(2,1)} fusion(bf16[1,512,1536]{2,1,0:T(8,128)(2,1)S(1)} %copy-done, bf16[64,8,1536]{2,1,0:T(8,128)(2,1)S(1)} %all_to_all.10, bf16[1,1536,512]{2,1,0:T(8,128)(2,1)} %param.24, f32[64,1,8,512]{3,2,0,1:T(8,128)} %fusion.6), kind=kOutput, calls=%fused_computation.1 | convolution fusion | flops 1612972032 | bytes 7340032 | tf_op jit(solution)/shard_map/senf,efd->send/dot_general | solution.py:104
  262.5 4.8 %all-to-all-start.1 = ((bf16[64,8,1536]{2,1,0:T(8,128)(2,1)}), bf16[64,8,1536]{2,1,0:T(8,128)(2,1)S(1)}, u32[]{:S(2)}, u32[]{:S(2)}) async-start(bf16[64,8,1536]{2,1,0:T(8,128)(2,1)} %convolution_convert_fusion), calls=%async_computation.1 | async-start | bytes 3145728 | tf_op jit(solution)/shard_map/all_to_all | solution.py:194
  267.3 0.8 reduce_sum.76
  268.1 1.6 mul.332
  269.6 0.9 copy.61
  271.1 0.8 copy.62
  271.9 0.7 compare_select_fusion
  273.2 2.3 copy.55
  275.5 1.3 fusion.25
  276.7 0.7 select_reduce_fusion
  277.5 0.7 copy.57
  278.2 144.7 %all-to-all-done.1 = bf16[64,8,1536]{2,1,0:T(8,128)(2,1)S(1)} async-done(((bf16[64,8,1536]{2,1,0:T(8,128)(2,1)}), bf16[64,8,1536]{2,1,0:T(8,128)(2,1)S(1)}, u32[]{:S(2)}, u32[]{:S(2)}) %all-to-all-start.1) | async-done | bytes 1572896 | tf_op jit(solution)/shard_map/all_to_all | solution.py:194
  423.0 2.3 gather_fusion
  425.2 2.3 gather.7
  427.5 4.0 multiply_reduce_fusion
  431.6 1.0 fusion.41
  (59 shorter events, 5.1 us)
Async XLA Ops:
  0.0 257.8 %copy-start = (bf16[1,512,1536]{2,1,0:T(8,128)(2,1)S(1)}, bf16[1,512,1536]{2,1,0:T(8,128)(2,1)}, u32[]{:S(2)}) copy-start(bf16[1,512,1536]{2,1,0:T(8,128)(2,1)} %param.25) | copy-start | bytes 4718596
  6.3 21.7 %copy-start.10 = (s32[1,128,2]{1,2,0:T(2,128)S(1)}, s32[1,128,2]{1,2,0:T(2,128)}, u32[]{:S(2)}) copy-start(s32[1,128,2]{1,2,0:T(2,128)} %param.22) | copy-start | bytes 3076
  7.7 28.0 %collective-permute-start.2 = (bf16[24,66,64]{1,2,0:T(8,128)(2,1)}, bf16[24,66,64]{1,2,0:T(8,128)(2,1)}, u32[]{:S(2)}, u32[]{:S(2)}) collective-permute-start(bf16[24,66,64]{1,2,0:T(8,128)(2,1)} %pad_maximum_fusion), channel_id=1, source_target_pairs={{0,192},{64,0},{128,64},{192,128},{256,448},{320,256},{384,320},{4... | collective-permute-start | bytes 608264 | tf_op jit(solution)/shard_map/ppermute | solution.py:30
  10.4 24.0 %collective-permute-start.1 = (bf16[24,66,64]{1,2,0:T(8,128)(2,1)}, bf16[24,66,64]{1,2,0:T(8,128)(2,1)}, u32[]{:S(2)}, u32[]{:S(2)}) collective-permute-start(bf16[24,66,64]{1,2,0:T(8,128)(2,1)} %pad_maximum_fusion), channel_id=1, source_target_pairs={{0,128},{64,192},{128,0},{192,64},{256,384},{320,448},{384,256},{4... | collective-permute-start | bytes 608264 | tf_op jit(solution)/shard_map/ppermute | solution.py:30
  26.1 10.0 %collective-permute-start = (bf16[24,66,64]{1,2,0:T(8,128)(2,1)}, bf16[24,66,64]{1,2,0:T(8,128)(2,1)}, u32[]{:S(2)}, u32[]{:S(2)}) collective-permute-start(bf16[24,66,64]{1,2,0:T(8,128)(2,1)} %pad_maximum_fusion), channel_id=1, source_target_pairs={{0,64},{64,128},{128,192},{192,0},{256,320},{320,384},{384,448},{4... | collective-permute-start | bytes 608264 | tf_op jit(solution)/shard_map/ppermute | solution.py:30
  29.4 237.9 %copy-start.8 = (s32[256]{0:T(256)}, s32[256]{0:T(256)S(1)}, u32[]{:S(2)}) copy-start(s32[256]{0:T(256)S(1)} %fusion.81) | copy-start | bytes 3076
  41.6 5.2 %copy-start.13 = (s32[128,2]{0,1:T(2,128)S(1)}, s32[128,2]{0,1:T(2,128)}, u32[]{:S(2)}) copy-start(s32[128,2]{0,1:T(2,128)} %copy.64) | copy-start | bytes 3076
  41.6 19.2 %copy-start.9 = (f32[128,24]{0,1:T(8,128)S(1)}, f32[128,24]{0,1:T(8,128)}, u32[]{:S(2)}) copy-start(f32[128,24]{0,1:T(8,128)} %get-tuple-element.25) | copy-start | bytes 36868
  42.2 11.5 %collective-permute-start.4 = (bf16[24,66,64]{1,2,0:T(8,128)(2,1)S(1)}, bf16[24,66,64]{1,2,0:T(8,128)(2,1)S(1)}, u32[]{:S(2)}, u32[]{:S(2)}) collective-permute-start(bf16[24,66,64]{1,2,0:T(8,128)(2,1)S(1)} %pad_maximum_fusion.1), channel_id=1, source_target_pairs={{0,512},{64,576},{128,640},{192,704},{256,768},{320,832},{384,896}... | collective-permute-start | bytes 608264 | tf_op jit(solution)/shard_map/ppermute | solution.py:34
  44.2 15.9 %collective-permute-start.3 = (bf16[24,66,64]{1,2,0:T(8,128)(2,1)S(1)}, bf16[24,66,64]{1,2,0:T(8,128)(2,1)S(1)}, u32[]{:S(2)}, u32[]{:S(2)}) collective-permute-start(bf16[24,66,64]{1,2,0:T(8,128)(2,1)S(1)} %pad_maximum_fusion.1), channel_id=1, source_target_pairs={{0,256},{64,320},{128,384},{192,448},{256,512},{320,576},{384,640}... | collective-permute-start | bytes 608264 | tf_op jit(solution)/shard_map/ppermute | solution.py:34
  47.6 13.2 %collective-permute-start.5 = (bf16[24,66,64]{1,2,0:T(8,128)(2,1)S(1)}, bf16[24,66,64]{1,2,0:T(8,128)(2,1)S(1)}, u32[]{:S(2)}, u32[]{:S(2)}) collective-permute-start(bf16[24,66,64]{1,2,0:T(8,128)(2,1)S(1)} %pad_maximum_fusion.1), channel_id=1, source_target_pairs={{0,768},{64,832},{128,896},{192,960},{1,769},{65,833},{129,897},{1... | collective-permute-start | bytes 608264 | tf_op jit(solution)/shard_map/ppermute | solution.py:34
  67.2 1.5 copy-start.6
  68.4 1.9 copy-start.1
  68.7 1.6 copy-start.5
  68.7 1.6 copy-start.12
  70.3 185.6 %copy-start.14 = (f32[128]{0:T(128)}, f32[128]{0:T(128)S(1)}, u32[]{:S(2)}) copy-start(f32[128]{0:T(128)S(1)} %add_rsqrt_fusion.1) | copy-start | bytes 1540
  71.0 184.9 %copy-start.15 = (bf16[1,1536,512]{2,1,0:T(8,128)(2,1)S(1)}, bf16[1,1536,512]{2,1,0:T(8,128)(2,1)}, u32[]{:S(2)}) copy-start(bf16[1,1536,512]{2,1,0:T(8,128)(2,1)} %param.23) | copy-start | bytes 4718596
  262.5 8.0 %copy-start.11 = (s32[1,128,2]{1,2,0:T(2,128)S(1)}, s32[1,128,2]{1,2,0:T(2,128)}, u32[]{:S(2)}) copy-start(s32[1,128,2]{1,2,0:T(2,128)} %param.22) | copy-start | bytes 3076
  262.5 160.4 %all-to-all-start.1 = ((bf16[64,8,1536]{2,1,0:T(8,128)(2,1)}), bf16[64,8,1536]{2,1,0:T(8,128)(2,1)S(1)}, u32[]{:S(2)}, u32[]{:S(2)}) async-start(bf16[64,8,1536]{2,1,0:T(8,128)(2,1)} %convolution_convert_fusion), calls=%async_computation.1 | async-start | bytes 3145728 | tf_op jit(solution)/shard_map/all_to_all | solution.py:194
  425.2 6.3 %copy-start.2 = (f32[1,128,1536]{2,1,0:T(8,128)S(1)}, f32[1,128,1536]{2,1,0:T(8,128)}, u32[]{:S(2)}) copy-start(f32[1,128,1536]{2,1,0:T(8,128)} %copy.55) | copy-start | bytes 2359300
  425.2 6.3 %copy-start.3 = (bf16[1,128,1536]{2,1,0:T(8,128)(2,1)S(1)}, bf16[1,128,1536]{2,1,0:T(8,128)(2,1)}, u32[]{:S(2)}) copy-start(bf16[1,128,1536]{2,1,0:T(8,128)(2,1)} %param.18) | copy-start | bytes 1179652
  427.5 4.0 copy-start.4
  427.5 4.0 copy-start.7

commit v6 on v4

--- a/solution.py
+++ b/solution.py
@@ -192,10 +192,13 @@
     arrived = lax.all_to_all(outgoing, "exp", split_axis=0, concat_axis=0, tiled=True)
     produced = apply_experts(arrived, gate_weight, up_weight, down_weight)
     returned = lax.all_to_all(produced, "exp", split_axis=0, concat_axis=0, tiled=True)
-    gathered = jnp.take(returned.reshape(-1, features), slot_index, axis=0).reshape(
-        tok_rows, top_count, features
-    )
-    mixture = jnp.sum(shares[:, :, None] * gathered.astype(jnp.float32), axis=1)
+    returned_rows = returned.reshape(-1, features)
+    slot_pairs = slot_index.reshape(tok_rows, top_count)
+    mixture = jnp.zeros((tok_rows, features), jnp.float32)
+    for choice in range(top_count):
+        picking = (slot_pairs[:, choice, None] == slot_labels[None, :]).astype(jnp.bfloat16)
+        gathered = jnp.dot(picking, returned_rows, preferred_element_type=jnp.float32)
+        mixture = mixture + shares[:, choice, None] * gathered
     return (h_float + mixture).astype(jnp.bfloat16).reshape(1, tok_rows, features)
 
 

time: 438 us -> 428 us (0.977)
  other arithmetic: 23.7 us -> 13.8 us
  local copies, waits for them, and re-layouts: 18.2 us -> 9.03 us
  waiting for transfers between devices: 157 us -> 164 us
    all_to_all x1, waiting for transfers between devices: 145 us -> 151 us  [on_device(): lax.all_to_all(produced, 'exp', split_axis=0, concat_axis=0, tiled=True)]
    gather x2 -> x0, local copies, waits for them, and re-layouts: 4.52 us -> none  [on_device(): jnp.take(returned.reshape(-1, features), slot_index, axis=0)]
  transfers between devices with their start and end apart: 7 -> 7, of which waited for: 5 -> 5; matrix products, arithmetic and copies ran while one was open for 4% -> 2% of each run, Pallas kernels for 0% -> 0%
where the time goes in v6:
time: 428 us; the launch traced here: 424 us
  blocking collectives  185 us (43%)
  waiting for transfers between devices  164 us (38%)
  starting transfers between devices  34 us (8%)
  matrix products  18 us (4%)
  other arithmetic  13.8 us (3%)
  local copies, waits for them, and re-layouts  9.03 us (2%)
    all_to_all x1, blocking collectives, on_device(): lax.all_to_all(outgoing, 'exp', split_axis=0, concat_axis=0, tiled=True)  185 us
    all_to_all x1, waiting for transfers between devices, on_device(): lax.all_to_all(produced, 'exp', split_axis=0, concat_axis=0, tiled=True)  151 us
    ppermute x3, starting transfers between devices, along_row(): return split(lax.ppermute(value, axis, pairs))  20.3 us
    ppermute x3, waiting for transfers between devices, along_col(): return split(lax.ppermute(value, axis, pairs))  9.86 us
    ppermute x3, starting transfers between devices, along_col(): return split(lax.ppermute(value, axis, pairs))  9.01 us
  transfers between devices with their start and end apart: 7, of which 5 were waited for; matrix products, arithmetic and copies ran while one was open for 2% of the time, Pallas kernels for 0%

profile of v6, /device:TPU:6, one launch (start us, length us, event | category | flops | bytes accessed | tf_op | source)
XLA Modules:
  0.0 423.9 jit_solution(7920967953396979907)
XLA Ops:
  0.0 1.1 reduce_window_sum.26
  1.1 0.2 slice_exponential_fusion
  1.4 1.2 copy.61
  2.6 1.2 copy.62
  3.8 0.8 fusion.107
  4.9 1.1 pad_maximum_fusion
  6.0 2.7 collective-permute-start.2
  8.7 15.6 %collective-permute-start.1 = (bf16[24,66,64]{1,2,0:T(8,128)(2,1)}, bf16[24,66,64]{1,2,0:T(8,128)(2,1)}, u32[]{:S(2)}, u32[]{:S(2)}) collective-permute-start(bf16[24,66,64]{1,2,0:T(8,128)(2,1)} %pad_maximum_fusion), channel_id=1, source_target_pairs={{0,128},{64,192},{128,0},{192,64},{256,384},{320,448},{384,256},{4... | collective-permute-start | bytes 608264 | tf_op jit(solution)/shard_map/ppermute | solution.py:30
  24.4 1.9 collective-permute-start
  26.5 0.1 eq.95
  26.6 0.1 eq.91
  26.8 0.6 reduce-window.6
  27.4 0.2 slice_reduce_fusion.2
  27.7 0.1 reduce_sum.64
  27.9 1.9 copy.60
  29.9 2.8 collective-permute-done.1
  32.7 1.2 fusion.102
  34.0 0.4 collective-permute-done
  34.4 1.5 fusion.99
  35.9 0.3 fusion.100
  36.1 0.3 convert_reduce_fusion.2
  36.4 2.7 fusion.37
  39.4 0.4 pad_maximum_fusion.1
  39.8 2.0 collective-permute-start.4
  41.7 2.6 collective-permute-start.3
  44.4 4.5 %collective-permute-start.5 = (bf16[24,66,64]{1,2,0:T(8,128)(2,1)S(1)}, bf16[24,66,64]{1,2,0:T(8,128)(2,1)S(1)}, u32[]{:S(2)}, u32[]{:S(2)}) collective-permute-start(bf16[24,66,64]{1,2,0:T(8,128)(2,1)S(1)} %pad_maximum_fusion.1), channel_id=1, source_target_pairs={{0,768},{64,832},{128,896},{192,960},{256,0},{320,64},{384,128},{4... | collective-permute-start | bytes 608264 | tf_op jit(solution)/shard_map/ppermute | solution.py:34
  48.9 5.4 %collective-permute-done.4 = bf16[24,66,64]{1,2,0:T(8,128)(2,1)S(1)} collective-permute-done((bf16[24,66,64]{1,2,0:T(8,128)(2,1)S(1)}, bf16[24,66,64]{1,2,0:T(8,128)(2,1)S(1)}, u32[]{:S(2)}, u32[]{:S(2)}) %collective-permute-start.4) | collective-permute-done | bytes 202784 | tf_op jit(solution)/shard_map/ppermute | solution.py:34
  54.3 4.5 %collective-permute-done.3 = bf16[24,66,64]{1,2,0:T(8,128)(2,1)S(1)} collective-permute-done((bf16[24,66,64]{1,2,0:T(8,128)(2,1)S(1)}, bf16[24,66,64]{1,2,0:T(8,128)(2,1)S(1)}, u32[]{:S(2)}, u32[]{:S(2)}) %collective-permute-start.3) | collective-permute-done | bytes 202784 | tf_op jit(solution)/shard_map/ppermute | solution.py:34
  58.8 0.6 fusion.93
  59.4 3.2 fusion.22
  62.7 3.2 multiply_reduce_fusion
  65.8 1.2 broadcast_multiply_fusion
  67.1 0.3 copy.64
  67.3 1.5 fusion.41
  68.9 0.6 copy-done.6
  69.4 0.6 fusion
  70.1 184.6 %all_to_all.10 = bf16[64,8,1536]{2,1,0:T(8,128)(2,1)S(1)} all-to-all(bf16[64,8,1536]{2,1,0:T(8,128)(2,1)S(1)} %fusion), channel_id=1, replica_groups=mesh['ctx'=16,'exp'=64] {'exp'}, dimensions={0} | all-to-all | bytes 3145728 | tf_op jit(solution)/shard_map/all_to_all | solution.py:192
  254.7 2.0 fusion.12
  256.7 4.7 %convolution_convert_fusion = bf16[64,8,1536]{2,1,0:T(8,128)(2,1)} fusion(bf16[1,512,1536]{2,1,0:T(8,128)(2,1)S(1)} %copy-done, bf16[64,8,1536]{2,1,0:T(8,128)(2,1)S(1)} %all_to_all.10, bf16[1,1536,512]{2,1,0:T(8,128)(2,1)} %param.24, f32[64,1,8,512]{3,2,0,1:T(8,128)} %fusion.12), kind=kOutput, calls=%fused_computation | convolution fusion | flops 1612972032 | bytes 7340032 | tf_op jit(solution)/shard_map/senf,efd->send/dot_general | solution.py:104
  261.3 4.7 %all-to-all-start.1 = ((bf16[64,8,1536]{2,1,0:T(8,128)(2,1)}), bf16[64,8,1536]{2,1,0:T(8,128)(2,1)S(1)}, u32[]{:S(2)}, u32[]{:S(2)}) async-start(bf16[64,8,1536]{2,1,0:T(8,128)(2,1)} %convolution_convert_fusion), calls=%async_computation.1 | async-start | bytes 3145728 | tf_op jit(solution)/shard_map/all_to_all | solution.py:194
  266.0 0.8 reduce_sum.63
  266.8 0.9 copy.66
  267.7 0.9 multiply_add_fusion
  268.6 0.7 slice_reduce_fusion
  269.2 1.3 fusion.31
  270.6 151.1 %all-to-all-done.1 = bf16[64,8,1536]{2,1,0:T(8,128)(2,1)S(1)} async-done(((bf16[64,8,1536]{2,1,0:T(8,128)(2,1)}), bf16[64,8,1536]{2,1,0:T(8,128)(2,1)S(1)}, u32[]{:S(2)}, u32[]{:S(2)}) %all-to-all-start.1) | async-done | bytes 1572896 | tf_op jit(solution)/shard_map/all_to_all | solution.py:194
  421.6 1.1 convolution_multiply_fusion.1
  422.7 1.2 fusion.4
  (37 shorter events, 1.1 us)
Async XLA Ops:
  0.0 256.7 %copy-start = (bf16[1,512,1536]{2,1,0:T(8,128)(2,1)S(1)}, bf16[1,512,1536]{2,1,0:T(8,128)(2,1)}, u32[]{:S(2)}) copy-start(bf16[1,512,1536]{2,1,0:T(8,128)(2,1)} %param.25) | copy-start | bytes 4718596
  4.6 21.7 %copy-start.5 = (s32[1,128,2]{1,2,0:T(2,128)S(1)}, s32[1,128,2]{1,2,0:T(2,128)}, u32[]{:S(2)}) copy-start(s32[1,128,2]{1,2,0:T(2,128)} %param.22) | copy-start | bytes 3076
  6.0 28.0 %collective-permute-start.2 = (bf16[24,66,64]{1,2,0:T(8,128)(2,1)}, bf16[24,66,64]{1,2,0:T(8,128)(2,1)}, u32[]{:S(2)}, u32[]{:S(2)}) collective-permute-start(bf16[24,66,64]{1,2,0:T(8,128)(2,1)} %pad_maximum_fusion), channel_id=1, source_target_pairs={{0,192},{64,0},{128,64},{192,128},{256,448},{320,256},{384,320},{4... | collective-permute-start | bytes 608264 | tf_op jit(solution)/shard_map/ppermute | solution.py:30
  8.7 24.0 %collective-permute-start.1 = (bf16[24,66,64]{1,2,0:T(8,128)(2,1)}, bf16[24,66,64]{1,2,0:T(8,128)(2,1)}, u32[]{:S(2)}, u32[]{:S(2)}) collective-permute-start(bf16[24,66,64]{1,2,0:T(8,128)(2,1)} %pad_maximum_fusion), channel_id=1, source_target_pairs={{0,128},{64,192},{128,0},{192,64},{256,384},{320,448},{384,256},{4... | collective-permute-start | bytes 608264 | tf_op jit(solution)/shard_map/ppermute | solution.py:30
  24.4 10.0 %collective-permute-start = (bf16[24,66,64]{1,2,0:T(8,128)(2,1)}, bf16[24,66,64]{1,2,0:T(8,128)(2,1)}, u32[]{:S(2)}, u32[]{:S(2)}) collective-permute-start(bf16[24,66,64]{1,2,0:T(8,128)(2,1)} %pad_maximum_fusion), channel_id=1, source_target_pairs={{0,64},{64,128},{128,192},{192,0},{256,320},{320,384},{384,448},{4... | collective-permute-start | bytes 608264 | tf_op jit(solution)/shard_map/ppermute | solution.py:30
  26.4 12.7 %copy-start.1 = (s32[1,128,2]{2,1,0:T(8,128)}, s32[1,128,2]{2,1,0:T(8,128)S(1)}, u32[]{:S(2)}) copy-start(s32[1,128,2]{2,1,0:T(8,128)S(1)} %copy.65) | copy-start | bytes 3076
  39.1 20.3 %copy-start.2 = (bf16[1,128,1536]{1,2,0:T(8,128)(2,1)S(1)}, bf16[1,128,1536]{1,2,0:T(8,128)(2,1)}, u32[]{:S(2)}) copy-start(bf16[1,128,1536]{1,2,0:T(8,128)(2,1)} %copy.60) | copy-start | bytes 1179652
  39.8 14.5 %collective-permute-start.4 = (bf16[24,66,64]{1,2,0:T(8,128)(2,1)S(1)}, bf16[24,66,64]{1,2,0:T(8,128)(2,1)S(1)}, u32[]{:S(2)}, u32[]{:S(2)}) collective-permute-start(bf16[24,66,64]{1,2,0:T(8,128)(2,1)S(1)} %pad_maximum_fusion.1), channel_id=1, source_target_pairs={{0,512},{64,576},{128,640},{192,704},{256,768},{320,832},{384,896}... | collective-permute-start | bytes 608264 | tf_op jit(solution)/shard_map/ppermute | solution.py:34
  41.7 17.0 %collective-permute-start.3 = (bf16[24,66,64]{1,2,0:T(8,128)(2,1)S(1)}, bf16[24,66,64]{1,2,0:T(8,128)(2,1)S(1)}, u32[]{:S(2)}, u32[]{:S(2)}) collective-permute-start(bf16[24,66,64]{1,2,0:T(8,128)(2,1)S(1)} %pad_maximum_fusion.1), channel_id=1, source_target_pairs={{0,256},{64,320},{128,384},{192,448},{256,512},{320,576},{384,640}... | collective-permute-start | bytes 608264 | tf_op jit(solution)/shard_map/ppermute | solution.py:34
  44.4 15.0 %collective-permute-start.5 = (bf16[24,66,64]{1,2,0:T(8,128)(2,1)S(1)}, bf16[24,66,64]{1,2,0:T(8,128)(2,1)S(1)}, u32[]{:S(2)}, u32[]{:S(2)}) collective-permute-start(bf16[24,66,64]{1,2,0:T(8,128)(2,1)S(1)} %pad_maximum_fusion.1), channel_id=1, source_target_pairs={{0,768},{64,832},{128,896},{192,960},{256,0},{320,64},{384,128},{4... | collective-permute-start | bytes 608264 | tf_op jit(solution)/shard_map/ppermute | solution.py:34
  65.8 1.5 copy-start.3
  67.0 2.4 copy-start.4
  68.8 0.6 copy-start.6
  70.1 184.6 %copy-start.7 = (bf16[1,1536,512]{2,1,0:T(8,128)(2,1)S(1)}, bf16[1,1536,512]{2,1,0:T(8,128)(2,1)}, u32[]{:S(2)}) copy-start(bf16[1,1536,512]{2,1,0:T(8,128)(2,1)} %param.23) | copy-start | bytes 4718596
  261.3 160.3 %all-to-all-start.1 = ((bf16[64,8,1536]{2,1,0:T(8,128)(2,1)}), bf16[64,8,1536]{2,1,0:T(8,128)(2,1)S(1)}, u32[]{:S(2)}, u32[]{:S(2)}) async-start(bf16[64,8,1536]{2,1,0:T(8,128)(2,1)} %convolution_convert_fusion), calls=%async_computation.1 | async-start | bytes 3145728 | tf_op jit(solution)/shard_map/all_to_all | solution.py:194
